TPU v7x, 256 devices: a whole 4x4x8 slice. The times are simulated.
256 devices in a mesh: gx: 32 (over x, z), gy: 8 (over y, core).
Axes of the slice: x: 4, y: 4, z: 8, core: 2. Of those that a mesh axis runs over, the one named last changes fastest.
Arguments:
- field: bfloat16 [3, 1, 48, 256, 1024], P(None, None, None, 'gx', 'gy'), may hold values from -6 to 6
- weight_x: bfloat16 [15, 48, 48], replicated, may hold values from -0.21875 to 0.21875
- weight_y: bfloat16 [15, 48, 48], replicated, may hold values from -0.21875 to 0.21875
- cotangent: bfloat16 [3, 1, 48, 256, 1024], P(None, None, None, 'gx', 'gy'), may hold values from -6 to 6
Outputs:
- output: bfloat16 [3, 1, 48, 256, 1024], P(None, None, None, 'gx', 'gy')
- field_grad: bfloat16 [3, 1, 48, 256, 1024], P(None, None, None, 'gx', 'gy')
- wx_grad: float32 [15, 48, 48], replicated
- wy_grad: float32 [15, 48, 48], replicated
All inputs are finite; a program needn't handle non-finite values.
Results may differ from a plain program's by a relative error of at most 0.0054.
Values may be sent and summed in bfloat16 or wider, within the bound.
No kernel may reach another device: no remote copies, remote signals or barrier semaphores. Data moves between devices by JAX's collectives and lax.ppermute only.
A program may use at most 64 MiB of HBM per device.

v0:
```python
import jax
import jax.numpy as jnp
from jax import lax
from jax.sharding import PartitionSpec as P


def with_halo(cells, sides, width):
    for axis, dim in sides:
        count = lax.axis_size(axis)
        ends = count - 1
        head = lax.slice_in_dim(cells, 0, width, axis=dim)
        tail = lax.slice_in_dim(cells, cells.shape[dim] - width, cells.shape[dim], axis=dim)
        cells = jnp.concatenate(
            [
                lax.ppermute(tail, axis, [(i, (i + 1) % count) for i in range(ends)]),
                cells,
                lax.ppermute(head, axis, [((i + 1) % count, i) for i in range(ends)]),
            ],
            axis=dim,
        )
    return cells


def conv_padded(padded, weight, dim):
    taps = weight.shape[0]
    length = padded.shape[dim] - taps + 1
    total = None
    for tap in range(taps):
        piece = lax.slice_in_dim(padded, tap, tap + length, axis=dim)
        term = jnp.einsum("bzcxy,co->bzoxy", piece, weight[tap], preferred_element_type=jnp.float32)
        total = term if total is None else total + term
    return total


def flipped(weight):
    return jnp.transpose(jnp.flip(weight, 0), (0, 2, 1))


def tap_products(padded, grads, taps, dim):
    length = grads.shape[dim]
    terms = []
    for tap in range(taps):
        piece = lax.slice_in_dim(padded, tap, tap + length, axis=dim)
        terms.append(
            jnp.einsum("bzcxy,bzoxy->co", piece, grads, preferred_element_type=jnp.float32)
        )
    return jnp.stack(terms)


def activate(pre):
    return jax.nn.gelu(pre.astype(jnp.float32)).astype(jnp.bfloat16)


def y_reach(values, half):
    return with_halo(values, (("gy", 4),), half)


def per_device(field, weight_x, weight_y, cotangent):
    taps = weight_x.shape[0]
    half = (taps - 1) // 2
    lines = lax.all_to_all(field, "gx", split_axis=4, concat_axis=3, tiled=True)
    lines_pad = jnp.pad(lines, ((0, 0), (0, 0), (0, 0), (half, half), (0, 0)))
    pre_lines = lax.optimization_barrier(conv_padded(lines_pad, weight_x, 3).astype(jnp.bfloat16))
    act_lines = activate(pre_lines)
    act, pre = (
        lax.all_to_all(act_lines, "gx", split_axis=3, concat_axis=4, tiled=True),
        lax.all_to_all(pre_lines, "gx", split_axis=3, concat_axis=4, tiled=True),
    )
    act_pad = y_reach(act, half)
    output = (field.astype(jnp.float32) + conv_padded(act_pad, weight_y, 4)).astype(jnp.bfloat16)
    grad_pad = y_reach(cotangent, half)
    act_grad = conv_padded(grad_pad, flipped(weight_y), 4)
    _, pull = jax.vjp(jax.nn.gelu, pre.astype(jnp.float32))
    pre_grad = pull(act_grad)[0].astype(jnp.bfloat16)
    wy_term = tap_products(act_pad, cotangent, taps, 4)
    paired = with_halo(jnp.stack((field, pre_grad)), (("gx", 4),), half)
    field_pad = paired[0]
    grad_xpad = paired[1]
    field_grad = (
        cotangent.astype(jnp.float32) + conv_padded(grad_xpad, flipped(weight_x), 3)
    ).astype(jnp.bfloat16)
    wx_term = tap_products(field_pad, pre_grad, taps, 3)
    wx_sum, wy_sum = lax.psum((wx_term, wy_term), ("gx", "gy"))
    count = (
        field.shape[0]
        * field.shape[1]
        * field.shape[3]
        * field.shape[4]
        * lax.axis_size("gx")
        * lax.axis_size("gy")
    )
    factor = 1.0 / jnp.sqrt(jnp.float32(count))
    return (output, field_grad, wx_sum * factor, wy_sum * factor)


def solution(mesh):
    in_specs = (P(None, None, None, "gx", "gy"), P(), P(), P(None, None, None, "gx", "gy"))
    out_specs = (P(None, None, None, "gx", "gy"), P(None, None, None, "gx", "gy"), P(), P())
    return jax.shard_map(
        per_device, mesh=mesh, in_specs=in_specs, out_specs=out_specs, check_vma=False
    )
```

profile of v0, /device:TPU:32, one launch (start us, length us, event | category | flops | bytes accessed | tf_op | source)
XLA Modules:
  0.0 375.7 jit_solution(10416243189057325038)
XLA Ops:
  7.2 1.6 copy.144
  8.8 1.7 reshape.644
  10.5 11.2 %all-to-all-start = ((bf16[32,2,2304]{2,1,0:T(2,128)(2,1)}), bf16[32,2,2304]{2,1,0:T(2,128)(2,1)S(1)}, u32[]{:S(2)}, u32[]{:S(2)}) async-start(bf16[32,2,2304]{2,1,0:T(2,128)(2,1)} %reshape.644), calls=%async_computation | async-start | bytes 589824 | tf_op jit(solution)/shard_map/all_to_all | solution.py:61
  22.0 1.3 collective-permute-start.3
  23.3 3.0 collective-permute-start.2
  26.6 0.7 reverse_bitcast_fusion
  27.3 0.8 copy.389
  28.0 0.4 fusion.110
  28.7 0.4 convolution_add_fusion.18
  29.1 0.4 convolution_add_fusion.17
  29.5 0.4 convolution_add_fusion.16
  29.9 0.4 convolution_add_fusion.15
  30.3 0.4 fusion.19
  31.1 1.1 fusion.6
  32.2 2.4 all-to-all-done
  34.6 0.8 reshape.645
  38.2 0.4 convolution_add_fusion.39
  41.0 0.6 copy.165
  41.6 1.7 reshape.646
  43.3 7.5 %all-to-all-start.1 = ((bf16[32,2,2304]{2,1,0:T(2,128)(2,1)}), bf16[32,2,2304]{2,1,0:T(2,128)(2,1)S(1)}, u32[]{:S(2)}, u32[]{:S(2)}) async-start(bf16[32,2,2304]{2,1,0:T(2,128)(2,1)} %reshape.646), calls=%async_computation.1 | async-start | bytes 589824 | tf_op jit(solution)/shard_map/all_to_all | solution.py:66
  50.9 1.0 fusion.5
  51.9 1.0 fusion.4
  52.9 1.0 fusion.3
  53.9 0.6 copy.196
  54.4 1.7 reshape.648
  56.2 7.0 %all-to-all-done.1 = bf16[32,2,2304]{2,1,0:T(2,128)(2,1)S(1)} async-done(((bf16[32,2,2304]{2,1,0:T(2,128)(2,1)}), bf16[32,2,2304]{2,1,0:T(2,128)(2,1)S(1)}, u32[]{:S(2)}, u32[]{:S(2)}) %all-to-all-start.1) | async-done | bytes 294944 | tf_op jit(solution)/shard_map/all_to_all | solution.py:66
  63.1 5.2 %all-to-all-start.2 = ((bf16[32,2,2304]{2,1,0:T(2,128)(2,1)}), bf16[32,2,2304]{2,1,0:T(2,128)(2,1)S(1)}, u32[]{:S(2)}, u32[]{:S(2)}) async-start(bf16[32,2,2304]{2,1,0:T(2,128)(2,1)} %reshape.648), calls=%async_computation.2 | async-start | bytes 589824 | tf_op jit(solution)/shard_map/all_to_all | solution.py:67
  68.4 1.9 fusion.2
  70.2 0.8 reshape.647
  71.3 0.5 copy.168
  71.8 0.5 copy.179
  72.3 0.9 fusion.299
  73.2 1.3 collective-permute-start.1
  74.5 3.3 collective-permute-start
  77.8 1.1 fusion.178
  78.9 3.5 all-to-all-done.2
  82.4 0.8 reshape.649
  83.6 1.3 copy.202
  84.9 1.9 fusion.65
  86.9 1.9 collective-permute-start.4
  88.9 4.2 %collective-permute-start.5 = (bf16[2,3,1,48,7,128]{5,3,4,1,2,0:T(8,128)(2,1)S(1)}, bf16[2,3,1,48,7,128]{5,3,4,1,2,0:T(8,128)(2,1)S(1)}, u32[]{:S(2)}, u32[]{:S(2)}) collective-permute-start(bf16[2,3,1,48,7,128]{5,3,4,1,2,0:T(8,128)(2,1)S(1)} %get-tuple-element.21), channel_id=1, source_target_pairs={{8,0},{16,8},{24,16},{32,24},{40,32},{48,40},{56,48},{64,56},{72,6... | collective-permute-start | bytes 1548296 | tf_op jit(solution)/shard_map/ppermute | solution.py:17
  93.7 0.4 fusion.39
  94.1 0.4 fusion.38
  94.8 0.4 fusion.36
  95.2 0.4 fusion.35
  95.8 0.4 fusion.185
  98.0 0.4 convolution_add_fusion.31
  98.4 0.4 convolution_add_fusion.30
  98.8 0.4 convolution_add_fusion.29
  99.2 0.4 convolution_add_fusion.28
  99.8 0.4 fusion
  100.2 0.4 convolution_add_fusion.26
  100.6 0.4 convolution_add_fusion.25
  101.0 0.4 convolution_add_fusion.24
  101.4 0.4 convolution_add_fusion.23
  101.8 0.4 convolution_add_fusion.22
  102.2 0.4 convolution_add_fusion.21
  102.7 0.4 fusion.23
  103.5 0.8 copy.220
  104.6 0.4 fusion.27
  105.0 0.7 copy-done.13
  113.1 0.8 copy.221
  113.9 253.0 %all-reduce.4.cloned.1.call-done = (f32[15,48,48]{2,1,0:T(8,128)}, f32[15,48,48]{2,1,0:T(8,128)}) async-done(((f32[15,48,48]{2,1,0:T(8,128)}, f32[15,48,48]{2,1,0:T(8,128)}), (f32[15,48,48]{2,1,0:T(8,128)}, f32[15,48,48]{2,1,0:T(8,128)})) %all-reduce.4.cloned.1.call-update) | async-done | bytes 276496 | tf_op jit(solution)/shard_map/psum | solution.py:83
  366.9 2.0 broadcast_multiply_fusion
  (110 shorter events, 18.1 us)
Async XLA Ops:
  7.2 14.5 %copy-start = (bf16[3,1,48,8,128]{4,3,2,1,0:T(8,128)(2,1)S(1)}, bf16[3,1,48,8,128]{4,3,2,1,0:T(8,128)(2,1)}, u32[]{:S(2)}) copy-start(bf16[3,1,48,8,128]{4,3,2,1,0:T(8,128)(2,1)} %param.7) | copy-start | bytes 884740
  8.8 17.6 %copy-start.9 = (bf16[15,48,48]{2,1,0:T(8,128)(2,1)S(1)}, bf16[15,48,48]{2,1,0:T(8,128)(2,1)}, u32[]{:S(2)}) copy-start(bf16[15,48,48]{2,1,0:T(8,128)(2,1)} %param.6) | copy-start | bytes 207364
  10.5 24.1 %all-to-all-start = ((bf16[32,2,2304]{2,1,0:T(2,128)(2,1)}), bf16[32,2,2304]{2,1,0:T(2,128)(2,1)S(1)}, u32[]{:S(2)}, u32[]{:S(2)}) async-start(bf16[32,2,2304]{2,1,0:T(2,128)(2,1)} %reshape.644), calls=%async_computation | async-start | bytes 589824 | tf_op jit(solution)/shard_map/all_to_all | solution.py:61
  21.7 4.9 %copy-start.8 = (bf16[15,48,48]{2,1,0:T(8,128)(2,1)S(1)}, bf16[15,48,48]{2,1,0:T(8,128)(2,1)}, u32[]{:S(2)}) copy-start(bf16[15,48,48]{2,1,0:T(8,128)(2,1)} %param.5) | copy-start | bytes 207364
  21.8 5.5 %copy-start.2 = (bf16[3,1,48,8,128]{4,3,2,1,0:T(8,128)(2,1)S(1)}, bf16[3,1,48,8,128]{4,3,2,1,0:T(8,128)(2,1)}, u32[]{:S(2)}) copy-start(bf16[3,1,48,8,128]{4,3,2,1,0:T(8,128)(2,1)} %param.4) | copy-start | bytes 884740
  22.0 8.7 %collective-permute-start.3 = (bf16[3,1,48,8,7]{4,2,3,0,1:T(8,128)(2,1)S(1)}, bf16[3,1,48,8,7]{4,2,3,0,1:T(8,128)(2,1)S(1)}, u32[]{:S(2)}, u32[]{:S(2)}) collective-permute-start(bf16[3,1,48,8,7]{4,2,3,0,1:T(8,128)(2,1)S(1)} %get-tuple-element.22), channel_id=1, source_target_pairs={{1,0},{2,1},{3,2},{4,3},{5,4},{6,5},{7,6},{9,8},{10,9},{11,10},{12... | collective-permute-start | bytes 48392 | tf_op jit(solution)/shard_map/ppermute | solution.py:17
  23.3 4.8 %collective-permute-start.2 = (bf16[3,1,48,8,7]{4,2,3,0,1:T(8,128)(2,1)S(1)}, bf16[3,1,48,8,7]{4,2,3,0,1:T(8,128)(2,1)S(1)}, u32[]{:S(2)}, u32[]{:S(2)}) collective-permute-start(bf16[3,1,48,8,7]{4,2,3,0,1:T(8,128)(2,1)S(1)} %get-tuple-element.23), channel_id=1, source_target_pairs={{0,1},{1,2},{2,3},{3,4},{4,5},{5,6},{6,7},{8,9},{9,10},{10,11},{11... | collective-permute-start | bytes 48392 | tf_op jit(solution)/shard_map/ppermute | solution.py:15
  26.4 4.7 %copy-start.12 = (bf16[15,48,48]{1,2,0:T(8,128)(2,1)}, bf16[15,48,48]{1,2,0:T(8,128)(2,1)S(1)}, u32[]{:S(2)}) copy-start(bf16[15,48,48]{1,2,0:T(8,128)(2,1)S(1)} %reverse_bitcast_fusion.1) | copy-start | bytes 207364
  40.8 10.0 %copy-start.5 = (f32[48,3,8,128]{3,0,2,1:T(8,128)S(1)}, f32[48,3,8,128]{3,0,2,1:T(8,128)}, u32[]{:S(2)}) copy-start(f32[48,3,8,128]{3,0,2,1:T(8,128)} %fusion.6) | copy-start | bytes 1769476
  43.3 19.8 %all-to-all-start.1 = ((bf16[32,2,2304]{2,1,0:T(2,128)(2,1)}), bf16[32,2,2304]{2,1,0:T(2,128)(2,1)S(1)}, u32[]{:S(2)}, u32[]{:S(2)}) async-start(bf16[32,2,2304]{2,1,0:T(2,128)(2,1)} %reshape.646), calls=%async_computation.1 | async-start | bytes 589824 | tf_op jit(solution)/shard_map/all_to_all | solution.py:66
  63.1 19.3 %all-to-all-start.2 = ((bf16[32,2,2304]{2,1,0:T(2,128)(2,1)}), bf16[32,2,2304]{2,1,0:T(2,128)(2,1)S(1)}, u32[]{:S(2)}, u32[]{:S(2)}) async-start(bf16[32,2,2304]{2,1,0:T(2,128)(2,1)} %reshape.648), calls=%async_computation.2 | async-start | bytes 589824 | tf_op jit(solution)/shard_map/all_to_all | solution.py:67
  68.3 298.6 %all-reduce.4.cloned.1.call-start = ((), (), s32[]{:S(2)}) async-start(), calls=%async_computation.3 | async-start | bytes 1474560 | tf_op jit(solution)/shard_map/psum | solution.py:83
  71.3 6.5 %copy-start.10 = (bf16[15,48,48]{2,1,0:T(8,128)(2,1)S(1)}, bf16[15,48,48]{2,1,0:T(8,128)(2,1)}, u32[]{:S(2)}) copy-start(bf16[15,48,48]{2,1,0:T(8,128)(2,1)} %param.6) | copy-start | bytes 207364
  72.3 11.0 %copy-start.6 = (bf16[3,48,8,128]{3,1,2,0:T(8,128)(2,1)}, bf16[3,48,8,128]{3,1,2,0:T(8,128)(2,1)S(1)}, u32[]{:S(2)}) copy-start(bf16[3,48,8,128]{3,1,2,0:T(8,128)(2,1)S(1)} %copy.179) | copy-start | bytes 884740
  73.2 23.0 %collective-permute-start.1 = (bf16[3,1,48,8,7]{4,2,3,0,1:T(8,128)(2,1)}, bf16[3,1,48,8,7]{4,2,3,0,1:T(8,128)(2,1)S(1)}, u32[]{:S(2)}, u32[]{:S(2)}) collective-permute-start(bf16[3,1,48,8,7]{4,2,3,0,1:T(8,128)(2,1)} %get-tuple-element.26), channel_id=1, source_target_pairs={{1,0},{2,1},{3,2},{4,3},{5,4},{6,5},{7,6},{9,8},{10,9},{11,10},{12... | collective-permute-start | bytes 48392 | tf_op jit(solution)/shard_map/ppermute | solution.py:17
  74.5 18.5 %collective-permute-start = (bf16[3,1,48,8,7]{4,2,3,0,1:T(8,128)(2,1)}, bf16[3,1,48,8,7]{4,2,3,0,1:T(8,128)(2,1)S(1)}, u32[]{:S(2)}, u32[]{:S(2)}) collective-permute-start(bf16[3,1,48,8,7]{4,2,3,0,1:T(8,128)(2,1)} %get-tuple-element.27), channel_id=1, source_target_pairs={{0,1},{1,2},{2,3},{3,4},{4,5},{5,6},{6,7},{8,9},{9,10},{10,11},{11... | collective-permute-start | bytes 48392 | tf_op jit(solution)/shard_map/ppermute | solution.py:15
  84.9 1.9 copy-start.1
  86.9 18.1 %collective-permute-start.4 = (bf16[2,3,1,48,7,128]{5,3,4,1,2,0:T(8,128)(2,1)S(1)}, bf16[2,3,1,48,7,128]{5,3,4,1,2,0:T(8,128)(2,1)S(1)}, u32[]{:S(2)}, u32[]{:S(2)}) collective-permute-start(bf16[2,3,1,48,7,128]{5,3,4,1,2,0:T(8,128)(2,1)S(1)} %get-tuple-element.20), channel_id=1, source_target_pairs={{0,8},{8,16},{16,24},{24,32},{32,40},{40,48},{48,56},{56,64},{64,7... | collective-permute-start | bytes 1548296 | tf_op jit(solution)/shard_map/ppermute | solution.py:15
  88.9 16.9 %collective-permute-start.5 = (bf16[2,3,1,48,7,128]{5,3,4,1,2,0:T(8,128)(2,1)S(1)}, bf16[2,3,1,48,7,128]{5,3,4,1,2,0:T(8,128)(2,1)S(1)}, u32[]{:S(2)}, u32[]{:S(2)}) collective-permute-start(bf16[2,3,1,48,7,128]{5,3,4,1,2,0:T(8,128)(2,1)S(1)} %get-tuple-element.21), channel_id=1, source_target_pairs={{8,0},{16,8},{24,16},{32,24},{40,32},{48,40},{56,48},{64,56},{72,6... | collective-permute-start | bytes 1548296 | tf_op jit(solution)/shard_map/ppermute | solution.py:17
  94.4 1.1 copy-start.7
  98.7 1.1 copy-start.4
  101.8 1.0 copy-start.3
  105.0 0.7 copy-start.13
  108.5 1.2 copy-start.11
  109.7 0.7 copy-start.14
Sparse Core Ops, SparseCore 0:
  113.0 253.8 all-reduce.3
where the time goes:
time: 379 us; the launch traced here: 376 us
  waiting for transfers between devices  266 us (70%)
  starting transfers between devices  39 us (10%)
  matrix products  33.7 us (9%)
  local copies, waits for them, and re-layouts  19.4 us (5%)
  between operations  15.2 us (4%)
    psum x1, waiting for transfers between devices, per_device(): wx_sum, wy_sum = lax.psum((wx_term, wy_term), ('gx', 'gy'))  253 us
    dot_general x60, matrix products, conv_padded(): jnp.einsum('bzcxy,co->bzoxy', piece, weight[tap], preferred_element_type=...  25.2 us
    unnamed x41, local copies, waits for them, and re-layouts  12.9 us
    all_to_all x1, starting transfers between devices, per_device(): lines = lax.all_to_all(field, 'gx', split_axis=4, concat_axis=3, tiled=True)  11.2 us
    dot_general x30, matrix products, tap_products(): jnp.einsum('bzcxy,bzoxy->co', piece, grads, preferred_element_type=jnp.fl...  8.47 us
    ppermute x3, starting transfers between devices, with_halo(): lax.ppermute(tail, axis, [(i, (i + 1) % count) for i in range(ends)])  8.28 us
  transfers between devices with their start and end apart: 10, of which 4 were waited for; matrix products, arithmetic and copies ran while one was open for 9% of the time, Pallas kernels for 0%

commit v1 on v0

--- a/solution.py
+++ b/solution.py
@@ -51,36 +51,44 @@
     return jax.nn.gelu(pre.astype(jnp.float32)).astype(jnp.bfloat16)
 
 
-def y_reach(values, half):
-    return with_halo(values, (("gy", 4),), half)
+def global_sum(parts, axes):
+    devices = 1
+    for axis in axes:
+        devices *= lax.axis_size(axis)
+    flat = jnp.concatenate([p.reshape(-1) for p in parts])
+    size = flat.shape[0]
+    chunk = -(-size // devices)
+    flat = jnp.pad(flat, (0, chunk * devices - size)).reshape(devices, chunk)
+    mine = jnp.sum(lax.all_to_all(flat, axes, 0, 0, tiled=True), axis=0)
+    full = lax.all_to_all(jnp.broadcast_to(mine[None], (devices, chunk)), axes, 0, 0, tiled=True)
+    full = full.reshape(-1)
+    out = []
+    start = 0
+    for p in parts:
+        out.append(full[start:start + p.size].reshape(p.shape))
+        start += p.size
+    return out
 
 
 def per_device(field, weight_x, weight_y, cotangent):
     taps = weight_x.shape[0]
     half = (taps - 1) // 2
-    lines = lax.all_to_all(field, "gx", split_axis=4, concat_axis=3, tiled=True)
-    lines_pad = jnp.pad(lines, ((0, 0), (0, 0), (0, 0), (half, half), (0, 0)))
-    pre_lines = lax.optimization_barrier(conv_padded(lines_pad, weight_x, 3).astype(jnp.bfloat16))
-    act_lines = activate(pre_lines)
-    act, pre = (
-        lax.all_to_all(act_lines, "gx", split_axis=3, concat_axis=4, tiled=True),
-        lax.all_to_all(pre_lines, "gx", split_axis=3, concat_axis=4, tiled=True),
-    )
-    act_pad = y_reach(act, half)
+    field_pad = with_halo(field, (("gx", 3),), half)
+    grad_pad = with_halo(cotangent, (("gy", 4),), half)
+    pre = lax.optimization_barrier(conv_padded(field_pad, weight_x, 3).astype(jnp.bfloat16))
+    act = activate(pre)
+    act_pad = with_halo(act, (("gy", 4),), half)
     output = (field.astype(jnp.float32) + conv_padded(act_pad, weight_y, 4)).astype(jnp.bfloat16)
-    grad_pad = y_reach(cotangent, half)
     act_grad = conv_padded(grad_pad, flipped(weight_y), 4)
     _, pull = jax.vjp(jax.nn.gelu, pre.astype(jnp.float32))
     pre_grad = pull(act_grad)[0].astype(jnp.bfloat16)
     wy_term = tap_products(act_pad, cotangent, taps, 4)
-    paired = with_halo(jnp.stack((field, pre_grad)), (("gx", 4),), half)
-    field_pad = paired[0]
-    grad_xpad = paired[1]
+    grad_xpad = with_halo(pre_grad, (("gx", 3),), half)
     field_grad = (
         cotangent.astype(jnp.float32) + conv_padded(grad_xpad, flipped(weight_x), 3)
     ).astype(jnp.bfloat16)
     wx_term = tap_products(field_pad, pre_grad, taps, 3)
-    wx_sum, wy_sum = lax.psum((wx_term, wy_term), ("gx", "gy"))
+    wx_sum, wy_sum = global_sum((wx_term, wy_term), ("gx", "gy"))
     count = (
         field.shape[0]
         * field.shape[1]

time: 379 us -> 135 us (0.36)
  the two profiles are of different devices: /device:TPU:32 before, /device:TPU:1 now
where the time goes in v1:
time: 135 us; the launch traced here: 134 us
  starting transfers between devices  46.6 us (35%)
  matrix products  46.6 us (35%)
  waiting for transfers between devices  24.8 us (18%)
  local copies, waits for them, and re-layouts  13 us (10%)
  other arithmetic  1.73 us (1%)
  between operations  1.39 us (1%)
    dot_general x30, matrix products, tap_products(): jnp.einsum('bzcxy,bzoxy->co', piece, grads, preferred_element_type=jnp.fl...  27 us
    dot_general x60, matrix products, conv_padded(): jnp.einsum('bzcxy,co->bzoxy', piece, weight[tap], preferred_element_type=...  19.6 us
    all_to_all x1, starting transfers between devices, global_sum(): mine = jnp.sum(lax.all_to_all(flat, axes, 0, 0, tiled=True), axis=0)  17.9 us
    all_to_all x1, waiting for transfers between devices, global_sum(): lax.all_to_all(jnp.broadcast_to(mine[None], (devices, chunk)), axes, 0, 0...  16.7 us
    ppermute x4, starting transfers between devices, with_halo(): lax.ppermute(tail, axis, [(i, (i + 1) % count) for i in range(ends)])  16.3 us
    all_to_all x1, waiting for transfers between devices, global_sum(): mine = jnp.sum(lax.all_to_all(flat, axes, 0, 0, tiled=True), axis=0)  8.02 us
    ppermute x4, starting transfers between devices, with_halo(): lax.ppermute(head, axis, [((i + 1) % count, i) for i in range(ends)])  6.74 us
    all_to_all x1, starting transfers between devices, global_sum(): lax.all_to_all(jnp.broadcast_to(mine[None], (devices, chunk)), axes, 0, 0...  5.7 us
  transfers between devices with their start and end apart: 10, of which 2 were waited for; matrix products, arithmetic and copies ran while one was open for 28% of the time, Pallas kernels for 0%

profile of v1, /device:TPU:1, one launch (start us, length us, event | category | flops | bytes accessed | tf_op | source)
XLA Modules:
  0.0 134.1 jit_solution(3091192867183541674)
XLA Ops:
  0.6 1.0 constant_dynamic-update-slice_fusion.5
  1.8 4.6 %collective-permute-start.4 = (bf16[3,1,48,8,7]{4,2,3,0,1:T(8,128)(2,1)S(1)}, bf16[3,1,48,8,7]{4,2,3,0,1:T(8,128)(2,1)S(1)}, u32[]{:S(2)}, u32[]{:S(2)}) collective-permute-start(bf16[3,1,48,8,7]{4,2,3,0,1:T(8,128)(2,1)S(1)} %get-tuple-element.21), channel_id=1, source_target_pairs={{0,1},{1,2},{2,3},{3,4},{4,5},{5,6},{6,7},{8,9},{9,10},{10,11},{11... | collective-permute-start | bytes 48392 | tf_op jit(solution)/shard_map/ppermute | solution.py:15
  6.4 1.9 %collective-permute-start.5 = (bf16[3,1,48,8,7]{4,2,3,0,1:T(8,128)(2,1)S(1)}, bf16[3,1,48,8,7]{4,2,3,0,1:T(8,128)(2,1)S(1)}, u32[]{:S(2)}, u32[]{:S(2)}) collective-permute-start(bf16[3,1,48,8,7]{4,2,3,0,1:T(8,128)(2,1)S(1)} %get-tuple-element.20), channel_id=1, source_target_pairs={{1,0},{2,1},{3,2},{4,3},{5,4},{6,5},{7,6},{9,8},{10,9},{11,10},{12... | collective-permute-start | bytes 48392 | tf_op jit(solution)/shard_map/ppermute | solution.py:17
  8.5 3.6 %collective-permute-start = (bf16[3,1,48,7,128]{4,2,3,0,1:T(8,128)(2,1)S(1)}, bf16[3,1,48,7,128]{4,2,3,0,1:T(8,128)(2,1)S(1)}, u32[]{:S(2)}, u32[]{:S(2)}) collective-permute-start(bf16[3,1,48,7,128]{4,2,3,0,1:T(8,128)(2,1)S(1)} %copy.354), channel_id=1, source_target_pairs={{0,8},{8,16},{16,24},{24,32},{32,40},{40,48},{48,56},{56,64},{64,7... | collective-permute-start | bytes 774152 | tf_op jit(solution)/shard_map/ppermute | solution.py:15
  12.2 1.4 %collective-permute-start.1 = (bf16[3,1,48,7,128]{4,2,3,0,1:T(8,128)(2,1)S(1)}, bf16[3,1,48,7,128]{4,2,3,0,1:T(8,128)(2,1)S(1)}, u32[]{:S(2)}, u32[]{:S(2)}) collective-permute-start(bf16[3,1,48,7,128]{4,2,3,0,1:T(8,128)(2,1)S(1)} %copy.355), channel_id=1, source_target_pairs={{8,0},{16,8},{24,16},{32,24},{40,32},{48,40},{56,48},{64,56},{72,6... | collective-permute-start | bytes 774152 | tf_op jit(solution)/shard_map/ppermute | solution.py:17
  13.9 0.7 copy-done.2
  23.6 0.6 fusion.61
  24.2 0.8 fusion.57
  25.1 0.9 fusion.317
  25.9 1.2 fusion.177
  27.2 0.8 fusion.56
  28.0 0.8 fusion.55
  28.8 0.8 fusion.54
  29.6 0.8 fusion.53
  30.5 0.8 fusion.52
  31.3 0.8 fusion.51
  32.1 0.8 fusion.50
  32.9 0.8 fusion.49
  33.8 0.8 fusion.48
  34.6 0.8 fusion.47
  35.4 0.8 fusion.46
  36.3 0.8 fusion.45
  37.1 0.8 fusion.44
  38.0 0.9 fusion.319
  38.9 4.6 %collective-permute-start.2 = (bf16[3,1,48,8,7]{4,2,3,0,1:T(8,128)(2,1)}, bf16[3,1,48,8,7]{4,2,3,0,1:T(8,128)(2,1)S(1)}, u32[]{:S(2)}, u32[]{:S(2)}) collective-permute-start(bf16[3,1,48,8,7]{4,2,3,0,1:T(8,128)(2,1)} %get-tuple-element.25), channel_id=1, source_target_pairs={{0,1},{1,2},{2,3},{3,4},{4,5},{5,6},{6,7},{8,9},{9,10},{10,11},{11... | collective-permute-start | bytes 48392 | tf_op jit(solution)/shard_map/ppermute | solution.py:15
  43.5 3.6 %collective-permute-start.6 = (bf16[3,1,48,7,128]{4,2,3,0,1:T(8,128)(2,1)}, bf16[3,1,48,7,128]{4,2,3,0,1:T(8,128)(2,1)S(1)}, u32[]{:S(2)}, u32[]{:S(2)}) collective-permute-start(bf16[3,1,48,7,128]{4,2,3,0,1:T(8,128)(2,1)} %get-tuple-element.19), channel_id=1, source_target_pairs={{0,8},{8,16},{16,24},{24,32},{32,40},{40,48},{48,56},{56,64},{64,7... | collective-permute-start | bytes 774152 | tf_op jit(solution)/shard_map/ppermute | solution.py:15
  47.3 0.8 fusion.43
  48.1 1.3 concatenate.92
  49.4 1.9 %collective-permute-start.3 = (bf16[3,1,48,8,7]{4,2,3,0,1:T(8,128)(2,1)}, bf16[3,1,48,8,7]{4,2,3,0,1:T(8,128)(2,1)S(1)}, u32[]{:S(2)}, u32[]{:S(2)}) collective-permute-start(bf16[3,1,48,8,7]{4,2,3,0,1:T(8,128)(2,1)} %get-tuple-element.24), channel_id=1, source_target_pairs={{1,0},{2,1},{3,2},{4,3},{5,4},{6,5},{7,6},{9,8},{10,9},{11,10},{12... | collective-permute-start | bytes 48392 | tf_op jit(solution)/shard_map/ppermute | solution.py:17
  51.3 1.5 %collective-permute-start.7 = (bf16[3,1,48,7,128]{4,2,3,0,1:T(8,128)(2,1)}, bf16[3,1,48,7,128]{4,2,3,0,1:T(8,128)(2,1)S(1)}, u32[]{:S(2)}, u32[]{:S(2)}) collective-permute-start(bf16[3,1,48,7,128]{4,2,3,0,1:T(8,128)(2,1)} %get-tuple-element.18), channel_id=1, source_target_pairs={{8,0},{16,8},{24,16},{32,24},{40,32},{48,40},{56,48},{64,56},{72,6... | collective-permute-start | bytes 774152 | tf_op jit(solution)/shard_map/ppermute | solution.py:17
  52.8 0.9 fusion.42
  53.7 1.0 fusion.41
  54.7 1.0 fusion.40
  55.7 1.0 fusion.39
  56.7 1.0 fusion.38
  57.6 1.0 fusion.37
  58.6 1.0 fusion.36
  59.6 1.0 fusion.35
  60.5 1.0 fusion.34
  61.5 1.0 fusion.33
  62.5 1.0 fusion.32
  63.4 1.0 fusion.31
  64.4 1.0 fusion.30
  65.4 1.0 fusion.29
  66.3 1.0 fusion.28
  67.3 1.3 concatenate.93
  68.6 1.2 copy.189
  69.8 17.9 %all-to-all-start = ((f32[256,1,270]{2,1,0:T(1,128)}), f32[256,1,270]{2,1,0:T(1,128)S(1)}, u32[]{:S(2)}, u32[]{:S(2)}) async-start(f32[256,1,270]{2,1,0:T(1,128)} %copy.189), calls=%async_computation | async-start | bytes 786432 | tf_op jit(solution)/shard_map/all_to_all | solution.py:62
  87.7 1.2 fusion.202
  90.8 0.7 copy-done.5
  91.8 0.4 convolution_add_fusion.25
  92.2 0.4 convolution_add_fusion.24
  93.4 0.4 convolution_add_fusion.21
  93.8 0.4 convolution_add_fusion.20
  94.2 0.4 fusion.24
  94.6 0.8 copy.190
  97.8 8.0 %all-to-all-done = f32[256,1,270]{2,1,0:T(1,128)S(1)} async-done(((f32[256,1,270]{2,1,0:T(1,128)}), f32[256,1,270]{2,1,0:T(1,128)S(1)}, u32[]{:S(2)}, u32[]{:S(2)}) %all-to-all-start) | async-done | bytes 276512 | tf_op jit(solution)/shard_map/all_to_all | solution.py:62
  106.2 1.0 broadcast_in_dim.2
  107.1 5.7 %all-to-all-start.1 = ((f32[256,1,270]{2,1,0:T(1,128)}), f32[256,1,270]{2,1,0:T(1,128)S(1)}, u32[]{:S(2)}, u32[]{:S(2)}) async-start(f32[256,1,270]{2,1,0:T(1,128)} %broadcast_in_dim.2), calls=%async_computation.1 | async-start | bytes 786432 | tf_op jit(solution)/shard_map/all_to_all | solution.py:63
  113.5 0.8 copy.191
  114.3 16.7 %all-to-all-done.1 = f32[256,1,270]{2,1,0:T(1,128)S(1)} async-done(((f32[256,1,270]{2,1,0:T(1,128)}), f32[256,1,270]{2,1,0:T(1,128)S(1)}, u32[]{:S(2)}, u32[]{:S(2)}) %all-to-all-start.1) | async-done | bytes 276512 | tf_op jit(solution)/shard_map/all_to_all | solution.py:63
  131.0 1.2 fusion.182
  132.2 0.9 mul.75
  133.2 0.9 mul.77
  (83 shorter events, 15.9 us)
Async XLA Ops:
  1.7 6.7 %copy-start.1 = (bf16[3,1,48,8,128]{4,3,2,1,0:T(8,128)(2,1)S(1)}, bf16[3,1,48,8,128]{4,3,2,1,0:T(8,128)(2,1)}, u32[]{:S(2)}) copy-start(bf16[3,1,48,8,128]{4,3,2,1,0:T(8,128)(2,1)} %param.4) | copy-start | bytes 884740
  1.8 12.8 %collective-permute-start.4 = (bf16[3,1,48,8,7]{4,2,3,0,1:T(8,128)(2,1)S(1)}, bf16[3,1,48,8,7]{4,2,3,0,1:T(8,128)(2,1)S(1)}, u32[]{:S(2)}, u32[]{:S(2)}) collective-permute-start(bf16[3,1,48,8,7]{4,2,3,0,1:T(8,128)(2,1)S(1)} %get-tuple-element.21), channel_id=1, source_target_pairs={{0,1},{1,2},{2,3},{3,4},{4,5},{5,6},{6,7},{8,9},{9,10},{10,11},{11... | collective-permute-start | bytes 48392 | tf_op jit(solution)/shard_map/ppermute | solution.py:15
  6.4 10.8 %collective-permute-start.5 = (bf16[3,1,48,8,7]{4,2,3,0,1:T(8,128)(2,1)S(1)}, bf16[3,1,48,8,7]{4,2,3,0,1:T(8,128)(2,1)S(1)}, u32[]{:S(2)}, u32[]{:S(2)}) collective-permute-start(bf16[3,1,48,8,7]{4,2,3,0,1:T(8,128)(2,1)S(1)} %get-tuple-element.20), channel_id=1, source_target_pairs={{1,0},{2,1},{3,2},{4,3},{5,4},{6,5},{7,6},{9,8},{10,9},{11,10},{12... | collective-permute-start | bytes 48392 | tf_op jit(solution)/shard_map/ppermute | solution.py:17
  8.5 10.6 %collective-permute-start = (bf16[3,1,48,7,128]{4,2,3,0,1:T(8,128)(2,1)S(1)}, bf16[3,1,48,7,128]{4,2,3,0,1:T(8,128)(2,1)S(1)}, u32[]{:S(2)}, u32[]{:S(2)}) collective-permute-start(bf16[3,1,48,7,128]{4,2,3,0,1:T(8,128)(2,1)S(1)} %copy.354), channel_id=1, source_target_pairs={{0,8},{8,16},{16,24},{24,32},{32,40},{40,48},{48,56},{56,64},{64,7... | collective-permute-start | bytes 774152 | tf_op jit(solution)/shard_map/ppermute | solution.py:15
  12.1 1.5 %copy-start.3 = (bf16[15,48,48]{2,1,0:T(8,128)(2,1)S(1)}, bf16[15,48,48]{2,1,0:T(8,128)(2,1)}, u32[]{:S(2)}) copy-start(bf16[15,48,48]{2,1,0:T(8,128)(2,1)} %param.6) | copy-start | bytes 207364
  12.2 1.5 %copy-start = (bf16[3,1,48,8,128]{4,3,2,1,0:T(8,128)(2,1)S(1)}, bf16[3,1,48,8,128]{4,3,2,1,0:T(8,128)(2,1)}, u32[]{:S(2)}) copy-start(bf16[3,1,48,8,128]{4,3,2,1,0:T(8,128)(2,1)} %param.7) | copy-start | bytes 884740
  12.2 9.3 %collective-permute-start.1 = (bf16[3,1,48,7,128]{4,2,3,0,1:T(8,128)(2,1)S(1)}, bf16[3,1,48,7,128]{4,2,3,0,1:T(8,128)(2,1)S(1)}, u32[]{:S(2)}, u32[]{:S(2)}) collective-permute-start(bf16[3,1,48,7,128]{4,2,3,0,1:T(8,128)(2,1)S(1)} %copy.355), channel_id=1, source_target_pairs={{8,0},{16,8},{24,16},{32,24},{40,32},{48,40},{56,48},{64,56},{72,6... | collective-permute-start | bytes 774152 | tf_op jit(solution)/shard_map/ppermute | solution.py:17
  13.7 0.9 copy-start.2
  38.9 13.9 %collective-permute-start.2 = (bf16[3,1,48,8,7]{4,2,3,0,1:T(8,128)(2,1)}, bf16[3,1,48,8,7]{4,2,3,0,1:T(8,128)(2,1)S(1)}, u32[]{:S(2)}, u32[]{:S(2)}) collective-permute-start(bf16[3,1,48,8,7]{4,2,3,0,1:T(8,128)(2,1)} %get-tuple-element.25), channel_id=1, source_target_pairs={{0,1},{1,2},{2,3},{3,4},{4,5},{5,6},{6,7},{8,9},{9,10},{10,11},{11... | collective-permute-start | bytes 48392 | tf_op jit(solution)/shard_map/ppermute | solution.py:15
  43.5 51.9 %collective-permute-start.6 = (bf16[3,1,48,7,128]{4,2,3,0,1:T(8,128)(2,1)}, bf16[3,1,48,7,128]{4,2,3,0,1:T(8,128)(2,1)S(1)}, u32[]{:S(2)}, u32[]{:S(2)}) collective-permute-start(bf16[3,1,48,7,128]{4,2,3,0,1:T(8,128)(2,1)} %get-tuple-element.19), channel_id=1, source_target_pairs={{0,8},{8,16},{16,24},{24,32},{32,40},{40,48},{48,56},{56,64},{64,7... | collective-permute-start | bytes 774152 | tf_op jit(solution)/shard_map/ppermute | solution.py:15
  49.4 11.1 %collective-permute-start.3 = (bf16[3,1,48,8,7]{4,2,3,0,1:T(8,128)(2,1)}, bf16[3,1,48,8,7]{4,2,3,0,1:T(8,128)(2,1)S(1)}, u32[]{:S(2)}, u32[]{:S(2)}) collective-permute-start(bf16[3,1,48,8,7]{4,2,3,0,1:T(8,128)(2,1)} %get-tuple-element.24), channel_id=1, source_target_pairs={{1,0},{2,1},{3,2},{4,3},{5,4},{6,5},{7,6},{9,8},{10,9},{11,10},{12... | collective-permute-start | bytes 48392 | tf_op jit(solution)/shard_map/ppermute | solution.py:17
  51.3 45.6 %collective-permute-start.7 = (bf16[3,1,48,7,128]{4,2,3,0,1:T(8,128)(2,1)}, bf16[3,1,48,7,128]{4,2,3,0,1:T(8,128)(2,1)S(1)}, u32[]{:S(2)}, u32[]{:S(2)}) collective-permute-start(bf16[3,1,48,7,128]{4,2,3,0,1:T(8,128)(2,1)} %get-tuple-element.18), channel_id=1, source_target_pairs={{8,0},{16,8},{24,16},{32,24},{40,32},{48,40},{56,48},{64,56},{72,6... | collective-permute-start | bytes 774152 | tf_op jit(solution)/shard_map/ppermute | solution.py:17
  69.8 36.1 %all-to-all-start = ((f32[256,1,270]{2,1,0:T(1,128)}), f32[256,1,270]{2,1,0:T(1,128)S(1)}, u32[]{:S(2)}, u32[]{:S(2)}) async-start(f32[256,1,270]{2,1,0:T(1,128)} %copy.189), calls=%async_computation | async-start | bytes 786432 | tf_op jit(solution)/shard_map/all_to_all | solution.py:62
  87.7 1.2 copy-start.4
  90.4 1.1 copy-start.5
  107.1 23.9 %all-to-all-start.1 = ((f32[256,1,270]{2,1,0:T(1,128)}), f32[256,1,270]{2,1,0:T(1,128)S(1)}, u32[]{:S(2)}, u32[]{:S(2)}) async-start(f32[256,1,270]{2,1,0:T(1,128)} %broadcast_in_dim.2), calls=%async_computation.1 | async-start | bytes 786432 | tf_op jit(solution)/shard_map/all_to_all | solution.py:63

commit v2 on v1

--- a/solution.py
+++ b/solution.py
@@ -22,14 +22,21 @@
 
 
 def conv_padded(padded, weight, dim):
-    taps = weight.shape[0]
-    length = padded.shape[dim] - taps + 1
-    total = None
-    for tap in range(taps):
-        piece = lax.slice_in_dim(padded, tap, tap + length, axis=dim)
-        term = jnp.einsum("bzcxy,co->bzoxy", piece, weight[tap], preferred_element_type=jnp.float32)
-        total = term if total is None else total + term
-    return total
+    b, z, c, x, y = padded.shape
+    cells = padded.reshape(b * z, c, x, y)
+    if dim == 4:
+        taps = weight.reshape((1,) + weight.shape)
+    else:
+        taps = weight.reshape((weight.shape[0], 1) + weight.shape[1:])
+    out = lax.conv_general_dilated(
+        cells,
+        taps,
+        (1, 1),
+        "VALID",
+        dimension_numbers=lax.ConvDimensionNumbers((0, 1, 2, 3), (3, 2, 0, 1), (0, 1, 2, 3)),
+        preferred_element_type=jnp.float32,
+    )
+    return out.reshape(b, z, out.shape[1], out.shape[2], out.shape[3])
 
 
 def flipped(weight):

time: 135 us -> 127 us (0.941)
  matrix products: 46.6 us -> 25 us
  local copies, waits for them, and re-layouts: 13 us -> 25.6 us
  waiting for transfers between devices: 24.8 us -> 18.6 us
  other arithmetic: 1.73 us -> 7.63 us
  starting transfers between devices: 46.6 us -> 48 us
    dot_general x60 -> x0, matrix products: 19.6 us -> none  [conv_padded(): jnp.einsum('bzcxy,co->bzoxy', piece, weight[tap], preferred_element_type=...]
    dot_general x30, matrix products: 27 us -> 8.49 us  [tap_products(): jnp.einsum('bzcxy,bzoxy->co', piece, grads, preferred_element_type=jnp.fl...]
    conv_general_dilated x0 -> x4, matrix products: none -> 16.5 us  [conv_padded(): lax.conv_general_dilated(cells, taps, (1, 1), 'VALID', dimension_numbers=...]
    unnamed x19 -> x40, local copies, waits for them, and re-layouts: 4.23 us -> 11.7 us
    all_to_all x1, waiting for transfers between devices: 16.7 us -> 11.8 us  [global_sum(): lax.all_to_all(jnp.broadcast_to(mine[None], (devices, chunk)), axes, 0, 0...]
    reshape x0 -> x3, local copies, waits for them, and re-layouts: none -> 2.17 us  [conv_padded(): cells = padded.reshape(b * z, c, x, y)]
    concatenate x2, local copies, waits for them, and re-layouts: 2.57 us -> 0.63 us  [global_sum(): flat = jnp.concatenate([p.reshape(-1) for p in parts])]
    convert_element_type x1 -> x3, other arithmetic: 0.22 us -> 2 us  [the longest x1 1.61 us: per_device(): pre_grad = pull(act_grad)[0].astype(jnp.bfloat16)]
  transfers between devices with their start and end apart: 10 -> 10, of which waited for: 2 -> 2; matrix products, arithmetic and copies ran while one was open for 28% -> 30% of each run, Pallas kernels for 0% -> 0%
where the time goes in v2:
time: 127 us; the launch traced here: 126 us
  starting transfers between devices  48 us (38%)
  local copies, waits for them, and re-layouts  25.6 us (20%)
  matrix products  25 us (20%)
  waiting for transfers between devices  18.6 us (15%)
  other arithmetic  7.63 us (6%)
  between operations  1.34 us (1%)
    all_to_all x1, starting transfers between devices, global_sum(): mine = jnp.sum(lax.all_to_all(flat, axes, 0, 0, tiled=True), axis=0)  17.5 us
    ppermute x4, starting transfers between devices, with_halo(): lax.ppermute(tail, axis, [(i, (i + 1) % count) for i in range(ends)])  17 us
    conv_general_dilated x4, matrix products, conv_padded(): lax.conv_general_dilated(cells, taps, (1, 1), 'VALID', dimension_numbers=...  16.5 us
    all_to_all x1, waiting for transfers between devices, global_sum(): lax.all_to_all(jnp.broadcast_to(mine[None], (devices, chunk)), axes, 0, 0...  11.8 us
    unnamed x40, local copies, waits for them, and re-layouts  11.7 us
    dot_general x30, matrix products, tap_products(): jnp.einsum('bzcxy,bzoxy->co', piece, grads, preferred_element_type=jnp.fl...  8.49 us
    all_to_all x1, starting transfers between devices, global_sum(): lax.all_to_all(jnp.broadcast_to(mine[None], (devices, chunk)), axes, 0, 0...  7.01 us
    all_to_all x1, waiting for transfers between devices, global_sum(): mine = jnp.sum(lax.all_to_all(flat, axes, 0, 0, tiled=True), axis=0)  6.72 us
  transfers between devices with their start and end apart: 10, of which 2 were waited for; matrix products, arithmetic and copies ran while one was open for 30% of the time, Pallas kernels for 0%

profile of v2, /device:TPU:1, one launch (start us, length us, event | category | flops | bytes accessed | tf_op | source)
XLA Modules:
  0.0 126.1 jit_solution(3694753236949346964)
XLA Ops:
  0.6 1.6 %copy.143 = bf16[3,1,48,8,128]{2,3,4,0,1:T(8,128)(2,1)S(1)} copy(bf16[3,1,48,8,128]{4,3,2,1,0:T(8,128)(2,1)} %param.7) | data formatting | bytes 589824 | tf_op args[3]
  2.2 4.6 %collective-permute-start.4 = (bf16[3,1,48,8,7]{2,3,4,0,1:T(8,128)(2,1)S(1)}, bf16[3,1,48,8,7]{2,3,4,0,1:T(8,128)(2,1)S(1)}, u32[]{:S(2)}, u32[]{:S(2)}) collective-permute-start(bf16[3,1,48,8,7]{2,3,4,0,1:T(8,128)(2,1)S(1)} %get-tuple-element.18), channel_id=1, source_target_pairs={{0,1},{1,2},{2,3},{3,4},{4,5},{5,6},{6,7},{8,9},{9,10},{10,11},{11... | collective-permute-start | bytes 48392 | tf_op jit(solution)/shard_map/ppermute | solution.py:15
  6.8 1.9 %collective-permute-start.5 = (bf16[3,1,48,8,7]{2,3,4,0,1:T(8,128)(2,1)S(1)}, bf16[3,1,48,8,7]{2,3,4,0,1:T(8,128)(2,1)S(1)}, u32[]{:S(2)}, u32[]{:S(2)}) collective-permute-start(bf16[3,1,48,8,7]{2,3,4,0,1:T(8,128)(2,1)S(1)} %get-tuple-element.19), channel_id=1, source_target_pairs={{1,0},{2,1},{3,2},{4,3},{5,4},{6,5},{7,6},{9,8},{10,9},{11,10},{12... | collective-permute-start | bytes 48392 | tf_op jit(solution)/shard_map/ppermute | solution.py:17
  8.8 1.1 fusion.164
  9.9 0.7 copy.261
  10.7 3.5 %collective-permute-start = (bf16[3,1,48,7,128]{4,2,3,0,1:T(8,128)(2,1)}, bf16[3,1,48,7,128]{4,2,3,0,1:T(8,128)(2,1)S(1)}, u32[]{:S(2)}, u32[]{:S(2)}) collective-permute-start(bf16[3,1,48,7,128]{4,2,3,0,1:T(8,128)(2,1)} %copy.261), channel_id=1, source_target_pairs={{0,8},{8,16},{16,24},{24,32},{32,40},{40,48},{48,56},{56,64},{64,7... | collective-permute-start | bytes 774152 | tf_op jit(solution)/shard_map/ppermute | solution.py:15
  14.2 0.7 copy.260
  15.0 1.4 %collective-permute-start.1 = (bf16[3,1,48,7,128]{4,2,3,0,1:T(8,128)(2,1)}, bf16[3,1,48,7,128]{4,2,3,0,1:T(8,128)(2,1)S(1)}, u32[]{:S(2)}, u32[]{:S(2)}) collective-permute-start(bf16[3,1,48,7,128]{4,2,3,0,1:T(8,128)(2,1)} %copy.260), channel_id=1, source_target_pairs={{8,0},{16,8},{24,16},{32,24},{40,32},{48,40},{56,48},{64,56},{72,6... | collective-permute-start | bytes 774152 | tf_op jit(solution)/shard_map/ppermute | solution.py:17
  16.4 1.3 %copy.133 = bf16[3,1,48,8,128]{2,4,0,3,1:T(8,128)(2,1)} copy(bf16[3,1,48,8,128]{4,3,2,1,0:T(8,128)(2,1)S(1)} %copy-done) | data formatting | bytes 589824 | tf_op args[0]
  17.7 1.3 %copy.129 = bf16[3,1,48,8,128]{2,3,4,0,1:T(8,128)(2,1)} copy(bf16[3,1,48,8,128]{4,3,2,1,0:T(8,128)(2,1)S(1)} %copy-done) | data formatting | bytes 589824 | tf_op args[0]
  19.0 0.4 copy.142
  19.4 0.7 rev.8
  20.6 0.4 fusion.7
  21.2 4.6 %fusion.19 = f32[8,24,18,48]{3,1,2,0:T(8,128)S(1)} fusion(bf16[48,8,3,8,32]{0,1,4,3,2:T(8,128)(2,1)S(1)} %fusion.7, pred[24,18]{0,1:T(8,128)(4,1)S(1)} %copy-done.13, bf16[15,48,48]{2,1,0:T(8,128)(2,1)S(1)} %rev.7), kind=kOutput, calls=%fused_computation.21 | convolution fusion | flops 239044608 | bytes 1322928 | tf_op jit(solution)/shard_map/conv_general_dilated | solution.py:31
  25.9 0.6 copy.147
  26.6 1.3 %copy.206 = f32[8,3,128,48]{2,3,0,1:T(8,128)} copy(f32[8,3,128,48]{3,0,2,1:T(8,128)S(1)} %slice.199) | data formatting | bytes 1179648
  27.9 0.4 copy.132
  28.3 1.1 copy.134
  29.5 1.6 %pad_maximum_fusion = bf16[3,1,48,22,128]{2,4,0,3,1:T(8,128)(2,1)S(1)} fusion(bf16[3,1,48,7,128]{2,4,0,3,1:T(8,128)(2,1)} %copy.134, bf16[3,1,48,8,128]{2,4,0,3,1:T(8,128)(2,1)S(1)} %copy-done.3, bf16[3,1,48,7,128]{2,4,0,3,1:T(8,128)(2,1)S(1)} %copy.132), kind=kLoop, calls=%fused_computation.3 | loop fusion | flops 811008 | bytes 1622016 | tf_op jit(solution)/shard_map/concatenate | solution.py:13
  31.1 3.2 %fusion.22 = bf16[8,24,16,48]{3,1,2,0:T(8,128)(2,1)S(1)} fusion(bf16[48,22,24,16]{0,3,2,1:T(8,128)(2,1)S(1)} %bitcast.467, bf16[15,48,48]{2,1,0:T(8,128)(2,1)S(1)} %copy-done.9), kind=kOutput, calls=%fused_computation.22 | convolution fusion | flops 212484096 | bytes 1175040 | tf_op jit(solution)/shard_map/conv_general_dilated | solution.py:31
  34.4 1.0 copy.138
  35.5 1.6 %fusion.58 = (bf16[3,1,48,8,128]{4,2,3,0,1:T(8,128)(2,1)S(1)}, bf16[3,1,48,8,128]{4,2,3,0,1:T(8,128)(2,1)S(1)}) fusion(bf16[3,1,48,8,128]{4,2,3,0,1:T(8,128)(2,1)} %bitcast.468, f32[8,3,128,48]{2,3,0,1:T(8,128)S(1)} %copy-done.4), kind=kLoop, calls=%fused_computation.117 | loop fusion | flops 3391488 | bytes 1474560 | tf_op jit(solution)/shard_map/convert_element_type | solution.py:91
  37.2 0.8 fusion.162
  41.3 3.9 %collective-permute-start.2 = (bf16[3,1,48,8,7]{4,2,3,0,1:T(8,128)(2,1)S(1)}, bf16[3,1,48,8,7]{4,2,3,0,1:T(8,128)(2,1)S(1)}, u32[]{:S(2)}, u32[]{:S(2)}) collective-permute-start(bf16[3,1,48,8,7]{4,2,3,0,1:T(8,128)(2,1)S(1)} %get-tuple-element.26), channel_id=1, source_target_pairs={{0,1},{1,2},{2,3},{3,4},{4,5},{5,6},{6,7},{8,9},{9,10},{10,11},{11... | collective-permute-start | bytes 48392 | tf_op jit(solution)/shard_map/ppermute | solution.py:15
  45.5 0.3 concatenate.62
  45.8 1.9 %collective-permute-start.3 = (bf16[3,1,48,8,7]{4,2,3,0,1:T(8,128)(2,1)S(1)}, bf16[3,1,48,8,7]{4,2,3,0,1:T(8,128)(2,1)S(1)}, u32[]{:S(2)}, u32[]{:S(2)}) collective-permute-start(bf16[3,1,48,8,7]{4,2,3,0,1:T(8,128)(2,1)S(1)} %get-tuple-element.27), channel_id=1, source_target_pairs={{1,0},{2,1},{3,2},{4,3},{5,4},{6,5},{7,6},{9,8},{10,9},{11,10},{12... | collective-permute-start | bytes 48392 | tf_op jit(solution)/shard_map/ppermute | solution.py:17
  47.7 5.0 %collective-permute-start.6 = (bf16[3,1,48,7,128]{4,2,3,0,1:T(8,128)(2,1)}, bf16[3,1,48,7,128]{4,2,3,0,1:T(8,128)(2,1)}, u32[]{:S(2)}, u32[]{:S(2)}) collective-permute-start(bf16[3,1,48,7,128]{4,2,3,0,1:T(8,128)(2,1)} %get-tuple-element.22), channel_id=1, source_target_pairs={{0,8},{8,16},{16,24},{24,32},{32,40},{40,48},{48,56},{56,64},{64,7... | collective-permute-start | bytes 774152 | tf_op jit(solution)/shard_map/ppermute | solution.py:15
  52.7 1.3 %collective-permute-start.7 = (bf16[3,1,48,7,128]{4,2,3,0,1:T(8,128)(2,1)}, bf16[3,1,48,7,128]{4,2,3,0,1:T(8,128)(2,1)}, u32[]{:S(2)}, u32[]{:S(2)}) collective-permute-start(bf16[3,1,48,7,128]{4,2,3,0,1:T(8,128)(2,1)} %get-tuple-element.23), channel_id=1, source_target_pairs={{8,0},{16,8},{24,16},{32,24},{40,32},{48,40},{56,48},{64,56},{72,6... | collective-permute-start | bytes 774152 | tf_op jit(solution)/shard_map/ppermute | solution.py:17
  54.3 0.4 fusion.38
  54.7 0.4 fusion.37
  55.0 0.4 fusion.36
  55.4 0.4 fusion.35
  55.8 0.4 fusion.34
  56.1 0.4 fusion.33
  56.5 0.3 fusion.32
  56.9 0.4 fusion.31
  57.2 0.4 fusion.30
  57.6 0.4 fusion.29
  58.0 0.4 fusion.28
  58.3 0.4 fusion.27
  58.7 0.4 fusion.26
  59.1 0.4 fusion.25
  59.4 0.3 concatenate.65
  59.8 1.1 copy.172
  60.9 17.5 %all-to-all-start = ((f32[256,1,270]{2,1,0:T(1,128)}), f32[256,1,270]{2,1,0:T(1,128)S(1)}, u32[]{:S(2)}, u32[]{:S(2)}) async-start(f32[256,1,270]{2,1,0:T(1,128)} %copy.172), calls=%async_computation | async-start | bytes 786432 | tf_op jit(solution)/shard_map/all_to_all | solution.py:69
  78.4 0.4 maximum_bitcast_fusion.2
  78.8 0.6 copy.207
  79.6 0.4 fusion.6
  80.0 0.5 copy-done.11
  80.5 3.8 %fusion.16 = f32[8,24,18,48]{3,1,2,0:T(8,128)S(1)} fusion(bf16[48,8,3,8,32]{0,1,4,3,2:T(8,128)(2,1)S(1)} %fusion.6, pred[24,18]{0,1:T(8,128)(4,1)S(1)} %copy-done.13, bf16[15,48,48]{2,1,0:T(8,128)(2,1)S(1)} %copy-done.11), kind=kOutput, calls=%fused_computation.20 | convolution fusion | flops 239044608 | bytes 1322928 | tf_op jit(solution)/shard_map/conv_general_dilated | solution.py:31
  84.4 0.6 copy.141
  84.9 0.5 copy-done.2
  85.6 1.2 copy.173
  86.9 1.2 maximum_bitcast_fusion.1
  88.0 1.8 %copy.149 = bf16[48,22,3,128]{0,3,2,1:T(8,128)(2,1)} copy(bf16[48,22,3,128]{3,0,1,2:T(8,128)(2,1)S(1)} %maximum_bitcast_fusion.1) | data formatting | bytes 1622016 | tf_op jit(solution)/shard_map/reshape | solution.py:26
  89.9 6.7 %all-to-all-done = f32[256,1,270]{2,1,0:T(1,128)S(1)} async-done(((f32[256,1,270]{2,1,0:T(1,128)}), f32[256,1,270]{2,1,0:T(1,128)S(1)}, u32[]{:S(2)}, u32[]{:S(2)}) %all-to-all-start) | async-done | bytes 276512 | tf_op jit(solution)/shard_map/all_to_all | solution.py:69
  96.9 0.9 broadcast_in_dim.2
  97.8 7.0 %all-to-all-start.1 = ((f32[256,1,270]{2,1,0:T(1,128)}), f32[256,1,270]{2,1,0:T(1,128)S(1)}, u32[]{:S(2)}, u32[]{:S(2)}) async-start(f32[256,1,270]{2,1,0:T(1,128)} %broadcast_in_dim.2), calls=%async_computation.1 | async-start | bytes 786432 | tf_op jit(solution)/shard_map/all_to_all | solution.py:70
  104.9 4.8 %fusion.2 = f32[8,24,16,48]{3,1,2,0:T(8,128)S(1)} fusion(bf16[48,22,24,16]{0,3,2,1:T(8,128)(2,1)} %bitcast.466, bf16[15,48,48]{2,1,0:T(8,128)(2,1)S(1)} %copy-done.12), kind=kOutput, calls=%fused_computation.4 | convolution fusion | flops 212336640 | bytes 1469952 | tf_op jit(solution)/shard_map/conv_general_dilated | solution.py:31
  110.2 1.0 copy.174
  111.2 11.8 %all-to-all-done.1 = f32[256,1,270]{2,1,0:T(1,128)S(1)} async-done(((f32[256,1,270]{2,1,0:T(1,128)}), f32[256,1,270]{2,1,0:T(1,128)S(1)}, u32[]{:S(2)}, u32[]{:S(2)}) %all-to-all-start.1) | async-done | bytes 276512 | tf_op jit(solution)/shard_map/all_to_all | solution.py:70
  123.1 1.2 fusion.125
  124.2 0.9 mul.75
  125.2 0.9 mul.77
  (68 shorter events, 6.0 us)
Async XLA Ops:
  0.6 15.8 %copy-start = (bf16[3,1,48,8,128]{4,3,2,1,0:T(8,128)(2,1)S(1)}, bf16[3,1,48,8,128]{4,3,2,1,0:T(8,128)(2,1)}, u32[]{:S(2)}) copy-start(bf16[3,1,48,8,128]{4,3,2,1,0:T(8,128)(2,1)} %param.4) | copy-start | bytes 884740
  2.2 17.9 %collective-permute-start.4 = (bf16[3,1,48,8,7]{2,3,4,0,1:T(8,128)(2,1)S(1)}, bf16[3,1,48,8,7]{2,3,4,0,1:T(8,128)(2,1)S(1)}, u32[]{:S(2)}, u32[]{:S(2)}) collective-permute-start(bf16[3,1,48,8,7]{2,3,4,0,1:T(8,128)(2,1)S(1)} %get-tuple-element.18), channel_id=1, source_target_pairs={{0,1},{1,2},{2,3},{3,4},{4,5},{5,6},{6,7},{8,9},{9,10},{10,11},{11... | collective-permute-start | bytes 48392 | tf_op jit(solution)/shard_map/ppermute | solution.py:15
  6.8 13.3 %collective-permute-start.5 = (bf16[3,1,48,8,7]{2,3,4,0,1:T(8,128)(2,1)S(1)}, bf16[3,1,48,8,7]{2,3,4,0,1:T(8,128)(2,1)S(1)}, u32[]{:S(2)}, u32[]{:S(2)}) collective-permute-start(bf16[3,1,48,8,7]{2,3,4,0,1:T(8,128)(2,1)S(1)} %get-tuple-element.19), channel_id=1, source_target_pairs={{1,0},{2,1},{3,2},{4,3},{5,4},{6,5},{7,6},{9,8},{10,9},{11,10},{12... | collective-permute-start | bytes 48392 | tf_op jit(solution)/shard_map/ppermute | solution.py:17
  9.9 9.0 %copy-start.1 = (bf16[3,1,48,8,128]{4,3,2,1,0:T(8,128)(2,1)S(1)}, bf16[3,1,48,8,128]{4,3,2,1,0:T(8,128)(2,1)}, u32[]{:S(2)}) copy-start(bf16[3,1,48,8,128]{4,3,2,1,0:T(8,128)(2,1)} %param.7) | copy-start | bytes 884740
  10.7 17.2 %collective-permute-start = (bf16[3,1,48,7,128]{4,2,3,0,1:T(8,128)(2,1)}, bf16[3,1,48,7,128]{4,2,3,0,1:T(8,128)(2,1)S(1)}, u32[]{:S(2)}, u32[]{:S(2)}) collective-permute-start(bf16[3,1,48,7,128]{4,2,3,0,1:T(8,128)(2,1)} %copy.261), channel_id=1, source_target_pairs={{0,8},{8,16},{16,24},{24,32},{32,40},{40,48},{48,56},{56,64},{64,7... | collective-permute-start | bytes 774152 | tf_op jit(solution)/shard_map/ppermute | solution.py:15
  14.2 5.2 %copy-start.10 = (bf16[15,48,48]{2,1,0:T(8,128)(2,1)S(1)}, bf16[15,48,48]{2,1,0:T(8,128)(2,1)}, u32[]{:S(2)}) copy-start(bf16[15,48,48]{2,1,0:T(8,128)(2,1)} %param.6) | copy-start | bytes 207364
  15.0 4.5 %copy-start.8 = (bf16[15,48,48]{2,1,0:T(8,128)(2,1)S(1)}, bf16[15,48,48]{2,1,0:T(8,128)(2,1)}, u32[]{:S(2)}) copy-start(bf16[15,48,48]{2,1,0:T(8,128)(2,1)} %param.5) | copy-start | bytes 207364
  15.0 13.3 %collective-permute-start.1 = (bf16[3,1,48,7,128]{4,2,3,0,1:T(8,128)(2,1)}, bf16[3,1,48,7,128]{4,2,3,0,1:T(8,128)(2,1)S(1)}, u32[]{:S(2)}, u32[]{:S(2)}) collective-permute-start(bf16[3,1,48,7,128]{4,2,3,0,1:T(8,128)(2,1)} %copy.260), channel_id=1, source_target_pairs={{8,0},{16,8},{24,16},{32,24},{40,32},{48,40},{56,48},{64,56},{72,6... | collective-permute-start | bytes 774152 | tf_op jit(solution)/shard_map/ppermute | solution.py:17
  20.6 0.7 copy-start.13
  27.9 1.6 %copy-start.3 = (bf16[3,1,48,8,128]{2,4,0,3,1:T(8,128)(2,1)S(1)}, bf16[3,1,48,8,128]{2,4,0,3,1:T(8,128)(2,1)}, u32[]{:S(2)}) copy-start(bf16[3,1,48,8,128]{2,4,0,3,1:T(8,128)(2,1)} %copy.133) | copy-start | bytes 884740
  28.3 2.8 %copy-start.6 = (bf16[3,1,48,7,128]{4,2,3,0,1:T(8,128)(2,1)}, bf16[3,1,48,7,128]{4,2,3,0,1:T(8,128)(2,1)S(1)}, u32[]{:S(2)}) copy-start(bf16[3,1,48,7,128]{4,2,3,0,1:T(8,128)(2,1)S(1)} %collective-permute-done.1) | copy-start | bytes 774148
  29.5 1.6 %copy-start.9 = (bf16[15,48,48]{2,1,0:T(8,128)(2,1)S(1)}, bf16[15,48,48]{2,1,0:T(8,128)(2,1)}, u32[]{:S(2)}) copy-start(bf16[15,48,48]{2,1,0:T(8,128)(2,1)} %param.5) | copy-start | bytes 207364
  34.3 1.3 copy-start.4
  38.5 1.4 %copy-start.7 = (bf16[3,1,48,7,128]{4,2,3,0,1:T(8,128)(2,1)S(1)}, bf16[3,1,48,7,128]{4,2,3,0,1:T(8,128)(2,1)}, u32[]{:S(2)}) copy-start(bf16[3,1,48,7,128]{4,2,3,0,1:T(8,128)(2,1)} %copy-done.6) | copy-start | bytes 774148
  41.3 12.6 %collective-permute-start.2 = (bf16[3,1,48,8,7]{4,2,3,0,1:T(8,128)(2,1)S(1)}, bf16[3,1,48,8,7]{4,2,3,0,1:T(8,128)(2,1)S(1)}, u32[]{:S(2)}, u32[]{:S(2)}) collective-permute-start(bf16[3,1,48,8,7]{4,2,3,0,1:T(8,128)(2,1)S(1)} %get-tuple-element.26), channel_id=1, source_target_pairs={{0,1},{1,2},{2,3},{3,4},{4,5},{5,6},{6,7},{8,9},{9,10},{10,11},{11... | collective-permute-start | bytes 48392 | tf_op jit(solution)/shard_map/ppermute | solution.py:15
  45.8 11.1 %collective-permute-start.3 = (bf16[3,1,48,8,7]{4,2,3,0,1:T(8,128)(2,1)S(1)}, bf16[3,1,48,8,7]{4,2,3,0,1:T(8,128)(2,1)S(1)}, u32[]{:S(2)}, u32[]{:S(2)}) collective-permute-start(bf16[3,1,48,8,7]{4,2,3,0,1:T(8,128)(2,1)S(1)} %get-tuple-element.27), channel_id=1, source_target_pairs={{1,0},{2,1},{3,2},{4,3},{5,4},{6,5},{7,6},{9,8},{10,9},{11,10},{12... | collective-permute-start | bytes 48392 | tf_op jit(solution)/shard_map/ppermute | solution.py:17
  47.7 39.1 %collective-permute-start.6 = (bf16[3,1,48,7,128]{4,2,3,0,1:T(8,128)(2,1)}, bf16[3,1,48,7,128]{4,2,3,0,1:T(8,128)(2,1)}, u32[]{:S(2)}, u32[]{:S(2)}) collective-permute-start(bf16[3,1,48,7,128]{4,2,3,0,1:T(8,128)(2,1)} %get-tuple-element.22), channel_id=1, source_target_pairs={{0,8},{8,16},{16,24},{24,32},{32,40},{40,48},{48,56},{56,64},{64,7... | collective-permute-start | bytes 774152 | tf_op jit(solution)/shard_map/ppermute | solution.py:15
  52.7 34.2 %collective-permute-start.7 = (bf16[3,1,48,7,128]{4,2,3,0,1:T(8,128)(2,1)}, bf16[3,1,48,7,128]{4,2,3,0,1:T(8,128)(2,1)}, u32[]{:S(2)}, u32[]{:S(2)}) collective-permute-start(bf16[3,1,48,7,128]{4,2,3,0,1:T(8,128)(2,1)} %get-tuple-element.23), channel_id=1, source_target_pairs={{8,0},{16,8},{24,16},{32,24},{40,32},{48,40},{56,48},{64,56},{72,6... | collective-permute-start | bytes 774152 | tf_op jit(solution)/shard_map/ppermute | solution.py:17
  55.4 1.1 copy-start.5
  60.9 35.7 %all-to-all-start = ((f32[256,1,270]{2,1,0:T(1,128)}), f32[256,1,270]{2,1,0:T(1,128)S(1)}, u32[]{:S(2)}, u32[]{:S(2)}) async-start(f32[256,1,270]{2,1,0:T(1,128)} %copy.172), calls=%async_computation | async-start | bytes 786432 | tf_op jit(solution)/shard_map/all_to_all | solution.py:69
  79.6 0.9 copy-start.11
  84.3 1.1 copy-start.2
  88.0 16.8 %copy-start.12 = (bf16[15,48,48]{2,1,0:T(8,128)(2,1)S(1)}, bf16[15,48,48]{2,1,0:T(8,128)(2,1)}, u32[]{:S(2)}) copy-start(bf16[15,48,48]{2,1,0:T(8,128)(2,1)} %rev.8) | copy-start | bytes 207364
  97.8 25.2 %all-to-all-start.1 = ((f32[256,1,270]{2,1,0:T(1,128)}), f32[256,1,270]{2,1,0:T(1,128)S(1)}, u32[]{:S(2)}, u32[]{:S(2)}) async-start(f32[256,1,270]{2,1,0:T(1,128)} %broadcast_in_dim.2), calls=%async_computation.1 | async-start | bytes 786432 | tf_op jit(solution)/shard_map/all_to_all | solution.py:70

commit v3 on v2

--- a/solution.py
+++ b/solution.py
@@ -58,16 +58,27 @@
     return jax.nn.gelu(pre.astype(jnp.float32)).astype(jnp.bfloat16)
 
 
-def global_sum(parts, axes):
-    devices = 1
-    for axis in axes:
-        devices *= lax.axis_size(axis)
+def tree_sum(values, axis):
+    count = lax.axis_size(axis)
+    step = 1
+    while step < count:
+        values = values + lax.ppermute(values, axis, [(i, i ^ step) for i in range(count)])
+        step *= 2
+    return values
+
+
+def global_sum(parts, scatter_axis, tree_axis, factor):
+    devices = lax.axis_size(scatter_axis)
+    lanes = 128
     flat = jnp.concatenate([p.reshape(-1) for p in parts])
     size = flat.shape[0]
-    chunk = -(-size // devices)
-    flat = jnp.pad(flat, (0, chunk * devices - size)).reshape(devices, chunk)
-    mine = jnp.sum(lax.all_to_all(flat, axes, 0, 0, tiled=True), axis=0)
-    full = lax.all_to_all(jnp.broadcast_to(mine[None], (devices, chunk)), axes, 0, 0, tiled=True)
+    rows = -(-size // (devices * lanes))
+    flat = jnp.pad(flat, (0, rows * devices * lanes - size)).reshape(devices, rows, lanes)
+    mine = jnp.sum(lax.all_to_all(flat, scatter_axis, 0, 0, tiled=True), axis=0)
+    mine = tree_sum(mine, tree_axis) * factor
+    full = lax.all_to_all(
+        jnp.broadcast_to(mine[None], (devices, rows, lanes)), scatter_axis, 0, 0, tiled=True
+    )
     full = full.reshape(-1)
     out = []
     start = 0
@@ -81,10 +92,11 @@
     taps = weight_x.shape[0]
     half = (taps - 1) // 2
     field_pad = with_halo(field, (("gx", 3),), half)
-    grad_pad = with_halo(cotangent, (("gy", 4),), half)
     pre = lax.optimization_barrier(conv_padded(field_pad, weight_x, 3).astype(jnp.bfloat16))
     act = activate(pre)
-    act_pad = with_halo(act, (("gy", 4),), half)
+    paired = with_halo(jnp.stack((act, cotangent)), (("gy", 5),), half)
+    act_pad = paired[0]
+    grad_pad = paired[1]
     output = (field.astype(jnp.float32) + conv_padded(act_pad, weight_y, 4)).astype(jnp.bfloat16)
     act_grad = conv_padded(grad_pad, flipped(weight_y), 4)
     _, pull = jax.vjp(jax.nn.gelu, pre.astype(jnp.float32))
@@ -95,7 +107,6 @@
         cotangent.astype(jnp.float32) + conv_padded(grad_xpad, flipped(weight_x), 3)
     ).astype(jnp.bfloat16)
     wx_term = tap_products(field_pad, pre_grad, taps, 3)
-    wx_sum, wy_sum = global_sum((wx_term, wy_term), ("gx", "gy"))
     count = (
         field.shape[0]
         * field.shape[1]
@@ -105,7 +116,8 @@
         * lax.axis_size("gy")
     )
     factor = 1.0 / jnp.sqrt(jnp.float32(count))
-    return (output, field_grad, wx_sum * factor, wy_sum * factor)
+    wx_sum, wy_sum = global_sum((wx_term, wy_term), "gx", "gy", factor)
+    return (output, field_grad, wx_sum, wy_sum)
 
 
 def solution(mesh):

time: 127 us -> 126 us (level)
  the two profiles are of different devices: /device:TPU:1 before, /device:TPU:32 now
where the time goes in v3:
time: 126 us; the launch traced here: 125 us
  starting transfers between devices  42.4 us (34%)
  matrix products  32.1 us (25%)
  local copies, waits for them, and re-layouts  25.9 us (21%)
  waiting for transfers between devices  17.4 us (14%)
  other arithmetic  5.59 us (4%)
  between operations  1.3 us (1%)
    conv_general_dilated x4, matrix products, conv_padded(): lax.conv_general_dilated(cells, taps, (1, 1), 'VALID', dimension_numbers=...  17.7 us
    dot_general x30, matrix products, tap_products(): jnp.einsum('bzcxy,bzoxy->co', piece, grads, preferred_element_type=jnp.fl...  14.5 us
    all_to_all x1, starting transfers between devices, global_sum(): mine = jnp.sum(lax.all_to_all(flat, scatter_axis, 0, 0, tiled=True), axis=0)  10.9 us
    unnamed x37, local copies, waits for them, and re-layouts  9.5 us
    ppermute x3, starting transfers between devices, tree_sum(): lax.ppermute(values, axis, [(i, i ^ step) for i in range(count)])  9.42 us
    ppermute x3, starting transfers between devices, with_halo(): lax.ppermute(tail, axis, [(i, (i + 1) % count) for i in range(ends)])  8.61 us
    all_to_all x1, waiting for transfers between devices, global_sum(): lax.all_to_all(jnp.broadcast_to(mine[None], (devices, rows, lanes)), scat...  7.84 us
    all_to_all x1, starting transfers between devices, global_sum(): lax.all_to_all(jnp.broadcast_to(mine[None], (devices, rows, lanes)), scat...  7.53 us
  transfers between devices with their start and end apart: 11, of which 5 were waited for; matrix products, arithmetic and copies ran while one was open for 21% of the time, Pallas kernels for 0%

profile of v3, /device:TPU:32, one launch (start us, length us, event | category | flops | bytes accessed | tf_op | source)
XLA Modules:
  0.0 124.8 jit_solution(12351092083301715277)
XLA Ops:
  0.7 1.2 fusion.103
  1.9 4.0 %collective-permute-start = (bf16[3,1,48,7,128]{4,2,3,0,1:T(8,128)(2,1)S(1)}, bf16[3,1,48,7,128]{4,2,3,0,1:T(8,128)(2,1)S(1)}, u32[]{:S(2)}, u32[]{:S(2)}) collective-permute-start(bf16[3,1,48,7,128]{4,2,3,0,1:T(8,128)(2,1)S(1)} %copy.267), channel_id=1, source_target_pairs={{0,8},{8,16},{16,24},{24,32},{32,40},{40,48},{48,56},{56,64},{64,7... | collective-permute-start | bytes 774152 | tf_op jit(solution)/shard_map/ppermute | solution.py:15
  5.9 2.0 %collective-permute-start.1 = (bf16[3,1,48,7,128]{4,2,3,0,1:T(8,128)(2,1)S(1)}, bf16[3,1,48,7,128]{4,2,3,0,1:T(8,128)(2,1)}, u32[]{:S(2)}, u32[]{:S(2)}) collective-permute-start(bf16[3,1,48,7,128]{4,2,3,0,1:T(8,128)(2,1)S(1)} %copy.266), channel_id=1, source_target_pairs={{8,0},{16,8},{24,16},{32,24},{40,32},{48,40},{56,48},{64,56},{72,6... | collective-permute-start | bytes 774152 | tf_op jit(solution)/shard_map/ppermute | solution.py:17
  8.0 0.4 copy.135
  8.5 3.4 %collective-permute-done = bf16[3,1,48,7,128]{4,2,3,0,1:T(8,128)(2,1)S(1)} collective-permute-done((bf16[3,1,48,7,128]{4,2,3,0,1:T(8,128)(2,1)S(1)}, bf16[3,1,48,7,128]{4,2,3,0,1:T(8,128)(2,1)S(1)}, u32[]{:S(2)}, u32[]{:S(2)}) %collective-permute-start) | collective-permute-done | bytes 258080 | tf_op jit(solution)/shard_map/ppermute | solution.py:15
  11.9 0.4 copy.134
  12.3 3.5 %collective-permute-done.1 = bf16[3,1,48,7,128]{4,2,3,0,1:T(8,128)(2,1)} collective-permute-done((bf16[3,1,48,7,128]{4,2,3,0,1:T(8,128)(2,1)S(1)}, bf16[3,1,48,7,128]{4,2,3,0,1:T(8,128)(2,1)}, u32[]{:S(2)}, u32[]{:S(2)}) %collective-permute-start.1) | collective-permute-done | bytes 258080 | tf_op jit(solution)/shard_map/ppermute | solution.py:17
  15.8 1.3 %copy.136 = bf16[3,1,48,7,128]{2,4,0,3,1:T(8,128)(2,1)S(1)} copy(bf16[3,1,48,7,128]{4,2,3,0,1:T(8,128)(2,1)} %collective-permute-done.1) | data formatting | bytes 516096 | tf_op jit(solution)/shard_map/ppermute | solution.py:17
  17.1 0.5 pad_maximum_fusion
  17.6 0.4 copy-done.4
  18.1 3.2 %fusion.22 = bf16[8,24,16,48]{3,1,2,0:T(8,128)(2,1)S(1)} fusion(bf16[48,22,24,16]{0,3,2,1:T(8,128)(2,1)S(1)} %bitcast.461, bf16[15,48,48]{2,1,0:T(8,128)(2,1)S(1)} %copy-done.4), kind=kOutput, calls=%fused_computation.22 | convolution fusion | flops 212484096 | bytes 1175040 | tf_op jit(solution)/shard_map/conv_general_dilated | solution.py:31
  22.1 0.4 copy.142
  22.5 1.3 %collective-permute-start.2 = (bf16[2,3,1,48,8,7]{3,4,5,2,1,0:T(8,128)(2,1)S(1)}, bf16[2,3,1,48,8,7]{3,4,5,2,1,0:T(8,128)(2,1)S(1)}, u32[]{:S(2)}, u32[]{:S(2)}) collective-permute-start(bf16[2,3,1,48,8,7]{3,4,5,2,1,0:T(8,128)(2,1)S(1)} %copy.142), channel_id=1, source_target_pairs={{0,1},{1,2},{2,3},{3,4},{4,5},{5,6},{6,7},{8,9},{9,10},{10,11},{11... | collective-permute-start | bytes 96776 | tf_op jit(solution)/shard_map/ppermute | solution.py:15
  23.8 0.4 copy.143
  24.2 1.5 %collective-permute-start.3 = (bf16[2,3,1,48,8,7]{3,4,5,2,1,0:T(8,128)(2,1)S(1)}, bf16[2,3,1,48,8,7]{3,4,5,2,1,0:T(8,128)(2,1)S(1)}, u32[]{:S(2)}, u32[]{:S(2)}) collective-permute-start(bf16[2,3,1,48,8,7]{3,4,5,2,1,0:T(8,128)(2,1)S(1)} %copy.143), channel_id=1, source_target_pairs={{1,0},{2,1},{3,2},{4,3},{5,4},{6,5},{7,6},{9,8},{10,9},{11,10},{12... | collective-permute-start | bytes 96776 | tf_op jit(solution)/shard_map/ppermute | solution.py:17
  25.7 0.7 constant_dynamic-update-slice_fusion.1
  26.5 0.8 constant_dynamic-update-slice_fusion.3
  27.3 1.0 constant_dynamic-update-slice_fusion.2
  28.3 0.8 copy-done.9
  29.1 0.4 copy.144
  29.5 0.4 copy.145
  29.9 0.7 pad_maximum_fusion.1
  30.6 1.2 slice_bitcast_fusion.2
  31.9 0.6 copy.211
  32.7 0.4 fusion.7
  33.4 4.6 %fusion.19 = f32[8,24,18,48]{3,1,2,0:T(8,128)S(1)} fusion(bf16[48,8,3,8,32]{0,1,4,3,2:T(8,128)(2,1)S(1)} %fusion.7, pred[24,18]{0,1:T(8,128)(4,1)S(1)} %copy-done.11, bf16[15,48,48]{2,1,0:T(8,128)(2,1)S(1)} %rev.7), kind=kOutput, calls=%fused_computation.21 | convolution fusion | flops 239044608 | bytes 1322928 | tf_op jit(solution)/shard_map/conv_general_dilated | solution.py:31
  38.0 0.6 copy.152
  38.7 0.5 copy.210
  39.2 0.4 fusion.58
  39.6 1.2 fusion.54
  40.8 1.2 fusion.53
  42.0 1.2 fusion.52
  43.2 1.2 fusion.51
  44.5 1.2 fusion.50
  45.6 1.2 fusion.49
  46.8 1.2 fusion.48
  50.2 0.3 fusion.38
  53.2 0.5 fusion.28
  54.8 0.8 reshape.223
  55.6 10.9 %all-to-all-start = ((f32[32,17,128]{2,1,0:T(8,128)}), f32[32,17,128]{2,1,0:T(8,128)S(1)}, u32[]{:S(2)}, u32[]{:S(2)}) async-start(f32[32,17,128]{2,1,0:T(8,128)} %reshape.223), calls=%async_computation | async-start | bytes 786432 | tf_op jit(solution)/shard_map/all_to_all | solution.py:77
  66.5 0.7 rev.8
  67.2 0.4 copy.149
  67.6 0.5 copy.131
  68.1 0.8 fusion.102
  68.9 3.4 %collective-permute-start.4 = (bf16[3,1,48,7,128]{4,2,3,0,1:T(8,128)(2,1)}, bf16[3,1,48,7,128]{4,2,3,0,1:T(8,128)(2,1)S(1)}, u32[]{:S(2)}, u32[]{:S(2)}) collective-permute-start(bf16[3,1,48,7,128]{4,2,3,0,1:T(8,128)(2,1)} %get-tuple-element.23), channel_id=1, source_target_pairs={{0,8},{8,16},{16,24},{24,32},{32,40},{40,48},{48,56},{56,64},{64,7... | collective-permute-start | bytes 774152 | tf_op jit(solution)/shard_map/ppermute | solution.py:15
  72.3 2.5 %collective-permute-start.5 = (bf16[3,1,48,7,128]{4,2,3,0,1:T(8,128)(2,1)}, bf16[3,1,48,7,128]{4,2,3,0,1:T(8,128)(2,1)}, u32[]{:S(2)}, u32[]{:S(2)}) collective-permute-start(bf16[3,1,48,7,128]{4,2,3,0,1:T(8,128)(2,1)} %get-tuple-element.24), channel_id=1, source_target_pairs={{8,0},{16,8},{24,16},{32,24},{40,32},{48,40},{56,48},{64,56},{72,6... | collective-permute-start | bytes 774152 | tf_op jit(solution)/shard_map/ppermute | solution.py:17
  74.8 1.6 %copy.212 = bf16[48,8,3,142]{0,1,3,2:T(8,128)(2,1)S(1)} copy(bf16[48,8,3,142]{3,0,1,2:T(8,128)(2,1)} %get-tuple-element.18) | data formatting | bytes 654336
  76.7 1.6 %fusion.6 = bf16[48,8,3,8,32]{0,1,4,3,2:T(8,128)(2,1)} fusion(bf16[48,8,3,7,14]{0,1,4,3,2:T(8,128)(2,1)S(1)} %slice.181, bf16[48,8,3,8,18]{0,1,4,3,2:T(8,128)(2,1)S(1)} %bitcast.449), kind=kLoop, calls=%fused_computation.8 | loop fusion | flops 1769472 | bytes 1147392 | tf_op jit(solution)/shard_map/conv_general_dilated | solution.py:31
  78.3 2.4 %all-to-all-done = f32[32,17,128]{2,1,0:T(8,128)S(1)} async-done(((f32[32,17,128]{2,1,0:T(8,128)}), f32[32,17,128]{2,1,0:T(8,128)S(1)}, u32[]{:S(2)}, u32[]{:S(2)}) %all-to-all-start) | async-done | bytes 278560 | tf_op jit(solution)/shard_map/all_to_all | solution.py:77
  80.7 2.6 %collective-permute-start.6 = (f32[17,128]{1,0:T(8,128)S(1)}, f32[17,128]{1,0:T(8,128)S(1)}, u32[]{:S(2)}, u32[]{:S(2)}) collective-permute-start(f32[17,128]{1,0:T(8,128)S(1)} %reduce_sum.9), channel_id=1, source_target_pairs={{0,1},{1,0},{2,3},{3,2},{4,5},{5,4},{6,7},{7,6},{8,9},{9,8},{10,11... | collective-permute-start | bytes 26120 | tf_op jit(solution)/shard_map/ppermute | solution.py:65
  83.4 5.0 %fusion.16 = f32[8,24,18,48]{3,1,2,0:T(8,128)S(1)} fusion(bf16[48,8,3,8,32]{0,1,4,3,2:T(8,128)(2,1)} %fusion.6, pred[24,18]{0,1:T(8,128)(4,1)S(1)} %copy-done.11, bf16[15,48,48]{2,1,0:T(8,128)(2,1)S(1)} %copy-done.7), kind=kOutput, calls=%fused_computation.20 | convolution fusion | flops 239044608 | bytes 1322928 | tf_op jit(solution)/shard_map/conv_general_dilated | solution.py:31
  88.4 0.6 copy.148
  89.0 3.3 %collective-permute-start.7 = (f32[17,128]{1,0:T(8,128)S(1)}, f32[17,128]{1,0:T(8,128)S(1)}, u32[]{:S(2)}, u32[]{:S(2)}) collective-permute-start(f32[17,128]{1,0:T(8,128)S(1)} %add.30), channel_id=1, source_target_pairs={{0,2},{1,3},{2,0},{3,1},{4,6},{5,7},{6,4},{7,5},{8,10},{9,11},{10,... | collective-permute-start | bytes 26120 | tf_op jit(solution)/shard_map/ppermute | solution.py:65
  92.4 1.2 copy.177
  93.9 3.5 %collective-permute-start.8 = (f32[17,128]{1,0:T(8,128)S(1)}, f32[17,128]{1,0:T(8,128)S(1)}, u32[]{:S(2)}, u32[]{:S(2)}) collective-permute-start(f32[17,128]{1,0:T(8,128)S(1)} %add.31), channel_id=1, source_target_pairs={{0,4},{1,5},{2,6},{3,7},{4,0},{5,1},{6,2},{7,3},{8,12},{9,13},{10,... | collective-permute-start | bytes 26120 | tf_op jit(solution)/shard_map/ppermute | solution.py:65
  97.5 1.0 maximum_bitcast_fusion
  98.5 1.8 %copy.154 = bf16[48,22,3,128]{0,3,2,1:T(8,128)(2,1)} copy(bf16[48,22,3,128]{3,0,1,2:T(8,128)(2,1)S(1)} %maximum_bitcast_fusion) | data formatting | bytes 1622016 | tf_op jit(solution)/shard_map/reshape | solution.py:26
  100.4 0.8 broadcast_in_dim.2
  101.2 7.5 %all-to-all-start.1 = ((f32[32,17,128]{2,1,0:T(8,128)}), f32[32,17,128]{2,1,0:T(8,128)S(1)}, u32[]{:S(2)}, u32[]{:S(2)}) async-start(f32[32,17,128]{2,1,0:T(8,128)} %broadcast_in_dim.2), calls=%async_computation.1 | async-start | bytes 786432 | tf_op jit(solution)/shard_map/all_to_all | solution.py:79
  108.7 4.8 %fusion.2 = f32[8,24,16,48]{3,1,2,0:T(8,128)S(1)} fusion(bf16[48,22,24,16]{0,3,2,1:T(8,128)(2,1)} %bitcast.460, bf16[15,48,48]{2,1,0:T(8,128)(2,1)S(1)} %copy-done.8), kind=kOutput, calls=%fused_computation.4 | convolution fusion | flops 212336640 | bytes 1469952 | tf_op jit(solution)/shard_map/conv_general_dilated | solution.py:31
  114.1 1.0 copy.178
  115.1 7.8 %all-to-all-done.1 = f32[32,17,128]{2,1,0:T(8,128)S(1)} async-done(((f32[32,17,128]{2,1,0:T(8,128)}), f32[32,17,128]{2,1,0:T(8,128)S(1)}, u32[]{:S(2)}, u32[]{:S(2)}) %all-to-all-start.1) | async-done | bytes 278560 | tf_op jit(solution)/shard_map/all_to_all | solution.py:79
  123.0 0.9 reshape.225
  123.9 0.9 reshape.226
  (75 shorter events, 8.8 us)
Async XLA Ops:
  0.6 7.3 %copy-start = (bf16[3,1,48,8,128]{4,3,2,1,0:T(8,128)(2,1)S(1)}, bf16[3,1,48,8,128]{4,3,2,1,0:T(8,128)(2,1)}, u32[]{:S(2)}) copy-start(bf16[3,1,48,8,128]{4,3,2,1,0:T(8,128)(2,1)} %param.4) | copy-start | bytes 884740
  0.6 7.8 %copy-start.1 = (bf16[3,1,48,8,128]{4,3,2,1,0:T(8,128)(2,1)S(1)}, bf16[3,1,48,8,128]{4,3,2,1,0:T(8,128)(2,1)}, u32[]{:S(2)}) copy-start(bf16[3,1,48,8,128]{4,3,2,1,0:T(8,128)(2,1)} %param.7) | copy-start | bytes 884740
  1.8 6.6 %copy-start.6 = (bf16[15,48,48]{2,1,0:T(8,128)(2,1)S(1)}, bf16[15,48,48]{2,1,0:T(8,128)(2,1)}, u32[]{:S(2)}) copy-start(bf16[15,48,48]{2,1,0:T(8,128)(2,1)} %param.6) | copy-start | bytes 207364
  1.9 10.0 %collective-permute-start = (bf16[3,1,48,7,128]{4,2,3,0,1:T(8,128)(2,1)S(1)}, bf16[3,1,48,7,128]{4,2,3,0,1:T(8,128)(2,1)S(1)}, u32[]{:S(2)}, u32[]{:S(2)}) collective-permute-start(bf16[3,1,48,7,128]{4,2,3,0,1:T(8,128)(2,1)S(1)} %copy.267), channel_id=1, source_target_pairs={{0,8},{8,16},{16,24},{24,32},{32,40},{40,48},{48,56},{56,64},{64,7... | collective-permute-start | bytes 774152 | tf_op jit(solution)/shard_map/ppermute | solution.py:15
  5.9 9.9 %collective-permute-start.1 = (bf16[3,1,48,7,128]{4,2,3,0,1:T(8,128)(2,1)S(1)}, bf16[3,1,48,7,128]{4,2,3,0,1:T(8,128)(2,1)}, u32[]{:S(2)}, u32[]{:S(2)}) collective-permute-start(bf16[3,1,48,7,128]{4,2,3,0,1:T(8,128)(2,1)S(1)} %copy.266), channel_id=1, source_target_pairs={{8,0},{16,8},{24,16},{32,24},{40,32},{48,40},{56,48},{64,56},{72,6... | collective-permute-start | bytes 774152 | tf_op jit(solution)/shard_map/ppermute | solution.py:17
  17.1 0.9 copy-start.4
  22.5 6.5 %collective-permute-start.2 = (bf16[2,3,1,48,8,7]{3,4,5,2,1,0:T(8,128)(2,1)S(1)}, bf16[2,3,1,48,8,7]{3,4,5,2,1,0:T(8,128)(2,1)S(1)}, u32[]{:S(2)}, u32[]{:S(2)}) collective-permute-start(bf16[2,3,1,48,8,7]{3,4,5,2,1,0:T(8,128)(2,1)S(1)} %copy.142), channel_id=1, source_target_pairs={{0,1},{1,2},{2,3},{3,4},{4,5},{5,6},{6,7},{8,9},{9,10},{10,11},{11... | collective-permute-start | bytes 96776 | tf_op jit(solution)/shard_map/ppermute | solution.py:15
  24.2 5.2 %collective-permute-start.3 = (bf16[2,3,1,48,8,7]{3,4,5,2,1,0:T(8,128)(2,1)S(1)}, bf16[2,3,1,48,8,7]{3,4,5,2,1,0:T(8,128)(2,1)S(1)}, u32[]{:S(2)}, u32[]{:S(2)}) collective-permute-start(bf16[2,3,1,48,8,7]{3,4,5,2,1,0:T(8,128)(2,1)S(1)} %copy.143), channel_id=1, source_target_pairs={{1,0},{2,1},{3,2},{4,3},{5,4},{6,5},{7,6},{9,8},{10,9},{11,10},{12... | collective-permute-start | bytes 96776 | tf_op jit(solution)/shard_map/ppermute | solution.py:17
  28.3 0.8 copy-start.9
  32.7 0.7 copy-start.11
  43.2 5.0 %copy-start.10 = (bf16[3,1,48,15,128]{4,2,3,0,1:T(8,128)(2,1)S(1)}, bf16[3,1,48,15,128]{4,2,3,0,1:T(8,128)(2,1)}, u32[]{:S(2)}) copy-start(bf16[3,1,48,15,128]{4,2,3,0,1:T(8,128)(2,1)} %copy-done.9) | copy-start | bytes 1658884
  48.9 1.1 copy-start.3
  54.2 12.3 %copy-start.5 = (bf16[15,48,48]{2,1,0:T(8,128)(2,1)S(1)}, bf16[15,48,48]{2,1,0:T(8,128)(2,1)}, u32[]{:S(2)}) copy-start(bf16[15,48,48]{2,1,0:T(8,128)(2,1)} %param.5) | copy-start | bytes 207364
  54.5 12.7 %copy-start.2 = (bf16[3,1,48,8,128]{4,3,2,1,0:T(8,128)(2,1)S(1)}, bf16[3,1,48,8,128]{4,3,2,1,0:T(8,128)(2,1)}, u32[]{:S(2)}) copy-start(bf16[3,1,48,8,128]{4,3,2,1,0:T(8,128)(2,1)} %param.7) | copy-start | bytes 884740
  55.6 25.1 %all-to-all-start = ((f32[32,17,128]{2,1,0:T(8,128)}), f32[32,17,128]{2,1,0:T(8,128)S(1)}, u32[]{:S(2)}, u32[]{:S(2)}) async-start(f32[32,17,128]{2,1,0:T(8,128)} %reshape.223), calls=%async_computation | async-start | bytes 786432 | tf_op jit(solution)/shard_map/all_to_all | solution.py:77
  68.9 28.5 %collective-permute-start.4 = (bf16[3,1,48,7,128]{4,2,3,0,1:T(8,128)(2,1)}, bf16[3,1,48,7,128]{4,2,3,0,1:T(8,128)(2,1)S(1)}, u32[]{:S(2)}, u32[]{:S(2)}) collective-permute-start(bf16[3,1,48,7,128]{4,2,3,0,1:T(8,128)(2,1)} %get-tuple-element.23), channel_id=1, source_target_pairs={{0,8},{8,16},{16,24},{24,32},{32,40},{40,48},{48,56},{56,64},{64,7... | collective-permute-start | bytes 774152 | tf_op jit(solution)/shard_map/ppermute | solution.py:15
  72.3 25.2 %collective-permute-start.5 = (bf16[3,1,48,7,128]{4,2,3,0,1:T(8,128)(2,1)}, bf16[3,1,48,7,128]{4,2,3,0,1:T(8,128)(2,1)}, u32[]{:S(2)}, u32[]{:S(2)}) collective-permute-start(bf16[3,1,48,7,128]{4,2,3,0,1:T(8,128)(2,1)} %get-tuple-element.24), channel_id=1, source_target_pairs={{8,0},{16,8},{24,16},{32,24},{40,32},{48,40},{56,48},{64,56},{72,6... | collective-permute-start | bytes 774152 | tf_op jit(solution)/shard_map/ppermute | solution.py:17
  76.7 6.7 %copy-start.7 = (bf16[15,48,48]{2,1,0:T(8,128)(2,1)S(1)}, bf16[15,48,48]{2,1,0:T(8,128)(2,1)}, u32[]{:S(2)}) copy-start(bf16[15,48,48]{2,1,0:T(8,128)(2,1)} %param.6) | copy-start | bytes 207364
  80.7 8.2 %collective-permute-start.6 = (f32[17,128]{1,0:T(8,128)S(1)}, f32[17,128]{1,0:T(8,128)S(1)}, u32[]{:S(2)}, u32[]{:S(2)}) collective-permute-start(f32[17,128]{1,0:T(8,128)S(1)} %reduce_sum.9), channel_id=1, source_target_pairs={{0,1},{1,0},{2,3},{3,2},{4,5},{5,4},{6,7},{7,6},{8,9},{9,8},{10,11... | collective-permute-start | bytes 26120 | tf_op jit(solution)/shard_map/ppermute | solution.py:65
  89.0 4.9 %collective-permute-start.7 = (f32[17,128]{1,0:T(8,128)S(1)}, f32[17,128]{1,0:T(8,128)S(1)}, u32[]{:S(2)}, u32[]{:S(2)}) collective-permute-start(f32[17,128]{1,0:T(8,128)S(1)} %add.30), channel_id=1, source_target_pairs={{0,2},{1,3},{2,0},{3,1},{4,6},{5,7},{6,4},{7,5},{8,10},{9,11},{10,... | collective-permute-start | bytes 26120 | tf_op jit(solution)/shard_map/ppermute | solution.py:65
  93.9 6.4 %collective-permute-start.8 = (f32[17,128]{1,0:T(8,128)S(1)}, f32[17,128]{1,0:T(8,128)S(1)}, u32[]{:S(2)}, u32[]{:S(2)}) collective-permute-start(f32[17,128]{1,0:T(8,128)S(1)} %add.31), channel_id=1, source_target_pairs={{0,4},{1,5},{2,6},{3,7},{4,0},{5,1},{6,2},{7,3},{8,12},{9,13},{10,... | collective-permute-start | bytes 26120 | tf_op jit(solution)/shard_map/ppermute | solution.py:65
  98.5 10.2 %copy-start.8 = (bf16[15,48,48]{2,1,0:T(8,128)(2,1)S(1)}, bf16[15,48,48]{2,1,0:T(8,128)(2,1)}, u32[]{:S(2)}) copy-start(bf16[15,48,48]{2,1,0:T(8,128)(2,1)} %rev.8) | copy-start | bytes 207364
  101.2 21.8 %all-to-all-start.1 = ((f32[32,17,128]{2,1,0:T(8,128)}), f32[32,17,128]{2,1,0:T(8,128)S(1)}, u32[]{:S(2)}, u32[]{:S(2)}) async-start(f32[32,17,128]{2,1,0:T(8,128)} %broadcast_in_dim.2), calls=%async_computation.1 | async-start | bytes 786432 | tf_op jit(solution)/shard_map/all_to_all | solution.py:79

commit v4 on v3

--- a/solution.py
+++ b/solution.py
@@ -22,22 +22,12 @@
 
 
 def conv_padded(padded, weight, dim):
-    b, z, c, x, y = padded.shape
-    cells = padded.reshape(b * z, c, x, y)
-    if dim == 4:
-        taps = weight.reshape((1,) + weight.shape)
-    else:
-        taps = weight.reshape((weight.shape[0], 1) + weight.shape[1:])
-    out = lax.conv_general_dilated(
-        cells,
-        taps,
-        (1, 1),
-        "VALID",
-        dimension_numbers=lax.ConvDimensionNumbers((0, 1, 2, 3), (3, 2, 0, 1), (0, 1, 2, 3)),
-        preferred_element_type=jnp.float32,
+    taps = weight.shape[0]
+    length = padded.shape[dim] - taps + 1
+    windows = jnp.stack(
+        [lax.slice_in_dim(padded, tap, tap + length, axis=dim) for tap in range(taps)]
     )
-    return out.reshape(b, z, out.shape[1], out.shape[2], out.shape[3])
-
+    return jnp.einsum("kbzcxy,kco->bzoxy", windows, weight, preferred_element_type=jnp.float32)
 
 def flipped(weight):
     return jnp.transpose(jnp.flip(weight, 0), (0, 2, 1))
@@ -45,14 +35,10 @@
 
 def tap_products(padded, grads, taps, dim):
     length = grads.shape[dim]
-    terms = []
-    for tap in range(taps):
-        piece = lax.slice_in_dim(padded, tap, tap + length, axis=dim)
-        terms.append(
-            jnp.einsum("bzcxy,bzoxy->co", piece, grads, preferred_element_type=jnp.float32)
-        )
-    return jnp.stack(terms)
-
+    windows = jnp.stack(
+        [lax.slice_in_dim(padded, tap, tap + length, axis=dim) for tap in range(taps)]
+    )
+    return jnp.einsum("kbzcxy,bzoxy->kco", windows, grads, preferred_element_type=jnp.float32)
 
 def activate(pre):
     return jax.nn.gelu(pre.astype(jnp.float32)).astype(jnp.bfloat16)

time: 126 us -> 117 us (0.929)
  matrix products: 32.1 us -> 13.2 us
  waiting for transfers between devices: 17.4 us -> 26.5 us
  other arithmetic: 5.59 us -> 12.2 us
  local copies, waits for them, and re-layouts: 25.9 us -> 21.6 us
    conv_general_dilated x4 -> x0, matrix products: 17.7 us -> none  [conv_padded(): lax.conv_general_dilated(cells, taps, (1, 1), 'VALID', dimension_numbers=...]
    unnamed x0 -> x14, other arithmetic: none -> 9.6 us
    ppermute x3, waiting for transfers between devices: 3.49 us -> 12.3 us  [with_halo(): lax.ppermute(head, axis, [((i + 1) % count, i) for i in range(ends)])]
    unnamed x37 -> x66, local copies, waits for them, and re-layouts: 9.5 us -> 14.3 us
    all_to_all x1, waiting for transfers between devices: 2.44 us -> 0.01 us  [global_sum(): mine = jnp.sum(lax.all_to_all(flat, scatter_axis, 0, 0, tiled=True), axis=0)]
    all_to_all x1, starting transfers between devices: 10.9 us -> 8.49 us  [global_sum(): mine = jnp.sum(lax.all_to_all(flat, scatter_axis, 0, 0, tiled=True), axis=0)]
    slice x3 -> x1, local copies, waits for them, and re-layouts: 2.44 us -> 0.4 us  [with_halo(): lax.slice_in_dim(cells, cells.shape[dim] - width, cells.shape[dim], axis=...]
    conv_general_dilated x2 -> x0, other arithmetic: 1.96 us -> none  [conv_padded(): lax.conv_general_dilated(cells, taps, (1, 1), 'VALID', dimension_numbers=...]
  transfers between devices with their start and end apart: 11 -> 11, of which waited for: 5 -> 8; matrix products, arithmetic and copies ran while one was open for 21% -> 20% of each run, Pallas kernels for 0% -> 0%
where the time goes in v4:
time: 117 us; the launch traced here: 116 us
  starting transfers between devices  41.2 us (35%)
  waiting for transfers between devices  26.5 us (23%)
  local copies, waits for them, and re-layouts  21.6 us (18%)
  matrix products  13.2 us (11%)
  other arithmetic  12.2 us (10%)
  between operations  1.24 us (1%)
    unnamed x66, local copies, waits for them, and re-layouts  14.3 us
    ppermute x3, waiting for transfers between devices, with_halo(): lax.ppermute(head, axis, [((i + 1) % count, i) for i in range(ends)])  12.3 us
    ppermute x3, starting transfers between devices, with_halo(): lax.ppermute(tail, axis, [(i, (i + 1) % count) for i in range(ends)])  10.2 us
    unnamed x14, other arithmetic  9.6 us
    all_to_all x1, waiting for transfers between devices, global_sum(): lax.all_to_all(jnp.broadcast_to(mine[None], (devices, rows, lanes)), scat...  9.2 us
    all_to_all x1, starting transfers between devices, global_sum(): lax.all_to_all(jnp.broadcast_to(mine[None], (devices, rows, lanes)), scat...  8.8 us
    all_to_all x1, starting transfers between devices, global_sum(): mine = jnp.sum(lax.all_to_all(flat, scatter_axis, 0, 0, tiled=True), axis=0)  8.49 us
    dot_general x4, matrix products, conv_padded(): jnp.einsum('kbzcxy,kco->bzoxy', windows, weight, preferred_element_type=j...  8.36 us
  transfers between devices with their start and end apart: 11, of which 8 were waited for; matrix products, arithmetic and copies ran while one was open for 20% of the time, Pallas kernels for 0%

profile of v4, /device:TPU:32, one launch (start us, length us, event | category | flops | bytes accessed | tf_op | source)
XLA Modules:
  0.0 115.8 jit_solution(16576797647056391458)
XLA Ops:
  0.6 1.2 %fusion.136 = (bf16[3,1,48,7,128]{4,3,2,1,0:T(8,128)(2,1)S(1)}, bf16[3,1,48,7,128]{4,3,2,1,0:T(8,128)(2,1)S(1)}) fusion(bf16[3,1,48,8,128]{4,3,2,1,0:T(8,128)(2,1)} %param.4), kind=kLoop, calls=%fused_computation.217 | loop fusion | bytes 1032192 | tf_op jit(solution)/shard_map/slice | solution.py:11
  1.9 3.8 %collective-permute-start = (bf16[3,1,48,7,128]{4,2,3,0,1:T(8,128)(2,1)S(1)}, bf16[3,1,48,7,128]{4,2,3,0,1:T(8,128)(2,1)S(1)}, u32[]{:S(2)}, u32[]{:S(2)}) collective-permute-start(bf16[3,1,48,7,128]{4,2,3,0,1:T(8,128)(2,1)S(1)} %copy.135), channel_id=1, source_target_pairs={{0,8},{8,16},{16,24},{24,32},{32,40},{40,48},{48,56},{56,64},{64,7... | collective-permute-start | bytes 774152 | tf_op jit(solution)/shard_map/ppermute | solution.py:15
  5.8 2.0 %collective-permute-start.1 = (bf16[3,1,48,7,128]{4,2,3,0,1:T(8,128)(2,1)S(1)}, bf16[3,1,48,7,128]{4,2,3,0,1:T(8,128)(2,1)S(1)}, u32[]{:S(2)}, u32[]{:S(2)}) collective-permute-start(bf16[3,1,48,7,128]{4,2,3,0,1:T(8,128)(2,1)S(1)} %copy.136), channel_id=1, source_target_pairs={{8,0},{16,8},{24,16},{32,24},{40,32},{48,40},{56,48},{64,56},{72,6... | collective-permute-start | bytes 774152 | tf_op jit(solution)/shard_map/ppermute | solution.py:17
  7.8 1.0 copy.137
  8.8 2.9 %collective-permute-done = bf16[3,1,48,7,128]{4,2,3,0,1:T(8,128)(2,1)S(1)} collective-permute-done((bf16[3,1,48,7,128]{4,2,3,0,1:T(8,128)(2,1)S(1)}, bf16[3,1,48,7,128]{4,2,3,0,1:T(8,128)(2,1)S(1)}, u32[]{:S(2)}, u32[]{:S(2)}) %collective-permute-start) | collective-permute-done | bytes 258080 | tf_op jit(solution)/shard_map/ppermute | solution.py:15
  11.7 1.1 constant_dynamic-update-slice_fusion.3
  13.2 2.3 %collective-permute-done.1 = bf16[3,1,48,7,128]{4,2,3,0,1:T(8,128)(2,1)S(1)} collective-permute-done((bf16[3,1,48,7,128]{4,2,3,0,1:T(8,128)(2,1)S(1)}, bf16[3,1,48,7,128]{4,2,3,0,1:T(8,128)(2,1)S(1)}, u32[]{:S(2)}, u32[]{:S(2)}) %collective-permute-start.1) | collective-permute-done | bytes 258080 | tf_op jit(solution)/shard_map/ppermute | solution.py:17
  15.9 2.1 %copy-done.2 = bf16[15,3,1,48,8,128]{5,3,0,4,1,2:T(8,128)(2,1)} copy-done((bf16[15,3,1,48,8,128]{5,3,0,4,1,2:T(8,128)(2,1)}, bf16[15,3,1,48,8,128]{5,3,0,4,1,2:T(8,128)(2,1)S(1)}, u32[]{:S(2)}) %copy-start.2) | copy-done | bytes 4423704
  18.0 0.9 fusion.27
  18.9 0.2 fusion.43
  19.1 0.2 slice_maximum_fusion
  19.4 0.4 copy.86
  19.8 1.3 %collective-permute-start.2 = (bf16[2,3,1,48,8,7]{3,4,5,2,1,0:T(8,128)(2,1)S(1)}, bf16[2,3,1,48,8,7]{3,4,5,2,1,0:T(8,128)(2,1)S(1)}, u32[]{:S(2)}, u32[]{:S(2)}) collective-permute-start(bf16[2,3,1,48,8,7]{3,4,5,2,1,0:T(8,128)(2,1)S(1)} %copy.86), channel_id=1, source_target_pairs={{0,1},{1,2},{2,3},{3,4},{4,5},{5,6},{6,7},{8,9},{9,10},{10,11},{11... | collective-permute-start | bytes 96776 | tf_op jit(solution)/shard_map/ppermute | solution.py:15
  21.1 0.4 copy.87
  21.5 1.5 %collective-permute-start.3 = (bf16[2,3,1,48,8,7]{3,4,5,2,1,0:T(8,128)(2,1)S(1)}, bf16[2,3,1,48,8,7]{3,4,5,2,1,0:T(8,128)(2,1)S(1)}, u32[]{:S(2)}, u32[]{:S(2)}) collective-permute-start(bf16[2,3,1,48,8,7]{3,4,5,2,1,0:T(8,128)(2,1)S(1)} %copy.87), channel_id=1, source_target_pairs={{1,0},{2,1},{3,2},{4,3},{5,4},{6,5},{7,6},{9,8},{10,9},{11,10},{12... | collective-permute-start | bytes 96776 | tf_op jit(solution)/shard_map/ppermute | solution.py:17
  23.1 0.4 copy.88
  23.5 3.0 %collective-permute-done.3 = bf16[2,3,1,48,8,7]{3,4,5,2,1,0:T(8,128)(2,1)S(1)} collective-permute-done((bf16[2,3,1,48,8,7]{3,4,5,2,1,0:T(8,128)(2,1)S(1)}, bf16[2,3,1,48,8,7]{3,4,5,2,1,0:T(8,128)(2,1)S(1)}, u32[]{:S(2)}, u32[]{:S(2)}) %collective-permute-start.3) | collective-permute-done | bytes 32288 | tf_op jit(solution)/shard_map/ppermute | solution.py:17
  26.5 0.4 copy.89
  26.9 0.7 pad_maximum_fusion
  27.8 0.2 fusion.112
  28.0 0.2 fusion.111
  28.2 0.2 fusion.110
  32.9 0.3 fusion.84
  33.3 2.0 %copy-done = bf16[15,3,1,48,8,128]{5,3,4,1,2,0:T(8,128)(2,1)} copy-done((bf16[15,3,1,48,8,128]{5,3,4,1,2,0:T(8,128)(2,1)}, bf16[15,3,1,48,8,128]{5,3,4,1,2,0:T(8,128)(2,1)S(1)}, u32[]{:S(2)}) %copy-start) | copy-done | bytes 4423704
  35.3 1.0 fusion.12
  36.3 0.4 fusion.33
  36.8 1.3 %fusion.21 = f32[15,48,48]{2,1,0:T(8,128)S(1)} fusion(bf16[15,3,1,48,8,128]{5,3,0,4,1,2:T(8,128)(2,1)S(1)} %bitcast.389, bf16[3,1,48,8,128]{4,2,3,0,1:T(8,128)(2,1)S(1)} %fusion.33), kind=kOutput, calls=%fused_computation.15 | convolution fusion | flops 212336640 | bytes 4856832 | tf_op jit(solution)/shard_map/kbzcxy,bzoxy->kco/dot_general | solution.py:41
  38.1 0.2 reshape.57
  38.4 3.5 %fusion.24 = f32[15,48,48]{2,1,0:T(8,128)S(1)} fusion(bf16[15,3,1,48,8,128]{5,3,4,1,2,0:T(8,128)(2,1)} %copy-done, bf16[3,48,8,128,1]{3,2,1,0,4:T(8,128)(2,1)S(1)} %bitcast.392), kind=kOutput, calls=%fused_computation.16 | convolution fusion | flops 212336640 | bytes 4856832 | tf_op jit(solution)/shard_map/kbzcxy,bzoxy->kco/dot_general | solution.py:41
  41.9 0.2 reshape.59
  42.1 5.0 %collective-permute-start.4 = (bf16[3,1,48,7,128]{4,2,3,0,1:T(8,128)(2,1)S(1)}, bf16[3,1,48,7,128]{4,2,3,0,1:T(8,128)(2,1)S(1)}, u32[]{:S(2)}, u32[]{:S(2)}) collective-permute-start(bf16[3,1,48,7,128]{4,2,3,0,1:T(8,128)(2,1)S(1)} %get-tuple-element.21), channel_id=1, source_target_pairs={{0,8},{8,16},{16,24},{24,32},{32,40},{40,48},{48,56},{56,64},{64,7... | collective-permute-start | bytes 774152 | tf_op jit(solution)/shard_map/ppermute | solution.py:15
  47.2 3.2 %fusion.4 = f32[3,8,128,48,1]{2,3,1,0,4:T(8,128)S(1)} fusion(bf16[15,3,1,48,8,128]{5,3,4,1,2,0:T(8,128)(2,1)} %copy-done, bf16[15,48,48]{2,1,0:T(8,128)(2,1)S(1)} %copy-done.5), kind=kOutput, calls=%fused_computation.4 | convolution fusion | flops 212336640 | bytes 5082624 | tf_op jit(solution)/shard_map/kbzcxy,kco->bzoxy/dot_general | solution.py:30
  50.4 0.8 reshape.60
  51.2 8.5 %all-to-all-start = ((f32[32,17,128]{2,1,0:T(8,128)}), f32[32,17,128]{2,1,0:T(8,128)S(1)}, u32[]{:S(2)}, u32[]{:S(2)}) async-start(f32[32,17,128]{2,1,0:T(8,128)} %reshape.60), calls=%async_computation | async-start | bytes 786432 | tf_op jit(solution)/shard_map/all_to_all | solution.py:63
  59.7 2.1 %collective-permute-start.5 = (bf16[3,1,48,7,128]{4,2,3,0,1:T(8,128)(2,1)S(1)}, bf16[3,1,48,7,128]{4,2,3,0,1:T(8,128)(2,1)S(1)}, u32[]{:S(2)}, u32[]{:S(2)}) collective-permute-start(bf16[3,1,48,7,128]{4,2,3,0,1:T(8,128)(2,1)S(1)} %get-tuple-element.20), channel_id=1, source_target_pairs={{8,0},{16,8},{24,16},{32,24},{40,32},{48,40},{56,48},{64,56},{72,6... | collective-permute-start | bytes 774152 | tf_op jit(solution)/shard_map/ppermute | solution.py:17
  61.9 0.8 copy.98
  62.7 0.7 fusion.67
  63.4 0.7 fusion.70
  64.2 0.8 fusion.73
  64.9 0.8 fusion.76
  65.7 0.7 fusion.79
  66.4 0.7 fusion.64
  67.1 0.7 fusion.83
  67.9 0.7 bitcast_dynamic-update-slice_fusion
  68.6 7.1 %collective-permute-done.5 = bf16[3,1,48,7,128]{4,2,3,0,1:T(8,128)(2,1)S(1)} collective-permute-done((bf16[3,1,48,7,128]{4,2,3,0,1:T(8,128)(2,1)S(1)}, bf16[3,1,48,7,128]{4,2,3,0,1:T(8,128)(2,1)S(1)}, u32[]{:S(2)}, u32[]{:S(2)}) %collective-permute-start.5) | collective-permute-done | bytes 258080 | tf_op jit(solution)/shard_map/ppermute | solution.py:17
  75.7 0.7 fusion.49
  76.4 0.8 fusion.52
  77.2 0.7 fusion.55
  77.9 0.7 fusion.58
  78.7 1.0 collective-permute-start.6
  79.6 0.7 fusion.61
  80.5 3.3 %collective-permute-start.7 = (f32[17,128]{1,0:T(8,128)S(1)}, f32[17,128]{1,0:T(8,128)S(1)}, u32[]{:S(2)}, u32[]{:S(2)}) collective-permute-start(f32[17,128]{1,0:T(8,128)S(1)} %add.30), channel_id=1, source_target_pairs={{0,2},{1,3},{2,0},{3,1},{4,6},{5,7},{6,4},{7,5},{8,10},{9,11},{10,... | collective-permute-start | bytes 26120 | tf_op jit(solution)/shard_map/ppermute | solution.py:51
  83.8 0.7 fusion.46
  84.5 0.9 collective-permute-done.7
  85.5 3.8 %collective-permute-start.8 = (f32[17,128]{1,0:T(8,128)S(1)}, f32[17,128]{1,0:T(8,128)S(1)}, u32[]{:S(2)}, u32[]{:S(2)}) collective-permute-start(f32[17,128]{1,0:T(8,128)S(1)} %add.31), channel_id=1, source_target_pairs={{0,4},{1,5},{2,6},{3,7},{4,0},{5,1},{6,2},{7,3},{8,12},{9,13},{10,... | collective-permute-start | bytes 26120 | tf_op jit(solution)/shard_map/ppermute | solution.py:51
  89.3 0.7 fusion.81
  90.0 0.9 collective-permute-done.8
  91.0 0.8 broadcast_in_dim.2
  91.8 8.8 %all-to-all-start.1 = ((f32[32,17,128]{2,1,0:T(8,128)}), f32[32,17,128]{2,1,0:T(8,128)S(1)}, u32[]{:S(2)}, u32[]{:S(2)}) async-start(f32[32,17,128]{2,1,0:T(8,128)} %broadcast_in_dim.2), calls=%async_computation.1 | async-start | bytes 786432 | tf_op jit(solution)/shard_map/all_to_all | solution.py:65
  100.6 3.3 %fusion = f32[3,8,128,48,1]{2,3,1,0,4:T(8,128)S(1)} fusion(bf16[15,3,1,48,8,128]{5,3,4,1,2,0:T(8,128)(2,1)} %fusion.81, bf16[15,48,48]{2,1,0:T(8,128)(2,1)S(1)} %rev.8), kind=kOutput, calls=%fused_computation | convolution fusion | flops 212336640 | bytes 5082624 | tf_op jit(solution)/shard_map/kbzcxy,kco->bzoxy/dot_general | solution.py:30
  103.9 0.8 copy.99
  104.7 9.2 %all-to-all-done.1 = f32[32,17,128]{2,1,0:T(8,128)S(1)} async-done(((f32[32,17,128]{2,1,0:T(8,128)}), f32[32,17,128]{2,1,0:T(8,128)S(1)}, u32[]{:S(2)}, u32[]{:S(2)}) %all-to-all-start.1) | async-done | bytes 278560 | tf_op jit(solution)/shard_map/all_to_all | solution.py:65
  113.9 0.9 reshape.62
  114.9 0.9 reshape.63
  (76 shorter events, 5.8 us)
Async XLA Ops:
  0.6 12.5 %copy-start.1 = (bf16[3,1,48,8,128]{4,3,2,1,0:T(8,128)(2,1)S(1)}, bf16[3,1,48,8,128]{4,3,2,1,0:T(8,128)(2,1)}, u32[]{:S(2)}) copy-start(bf16[3,1,48,8,128]{4,3,2,1,0:T(8,128)(2,1)} %param.4) | copy-start | bytes 884740
  1.9 9.9 %collective-permute-start = (bf16[3,1,48,7,128]{4,2,3,0,1:T(8,128)(2,1)S(1)}, bf16[3,1,48,7,128]{4,2,3,0,1:T(8,128)(2,1)S(1)}, u32[]{:S(2)}, u32[]{:S(2)}) collective-permute-start(bf16[3,1,48,7,128]{4,2,3,0,1:T(8,128)(2,1)S(1)} %copy.135), channel_id=1, source_target_pairs={{0,8},{8,16},{16,24},{24,32},{32,40},{40,48},{48,56},{56,64},{64,7... | collective-permute-start | bytes 774152 | tf_op jit(solution)/shard_map/ppermute | solution.py:15
  5.8 9.8 %collective-permute-start.1 = (bf16[3,1,48,7,128]{4,2,3,0,1:T(8,128)(2,1)S(1)}, bf16[3,1,48,7,128]{4,2,3,0,1:T(8,128)(2,1)S(1)}, u32[]{:S(2)}, u32[]{:S(2)}) collective-permute-start(bf16[3,1,48,7,128]{4,2,3,0,1:T(8,128)(2,1)S(1)} %copy.136), channel_id=1, source_target_pairs={{8,0},{16,8},{24,16},{32,24},{40,32},{48,40},{56,48},{64,56},{72,6... | collective-permute-start | bytes 774152 | tf_op jit(solution)/shard_map/ppermute | solution.py:17
  12.9 5.1 %copy-start.4 = (bf16[15,48,48]{2,1,0:T(8,128)(2,1)S(1)}, bf16[15,48,48]{2,1,0:T(8,128)(2,1)}, u32[]{:S(2)}) copy-start(bf16[15,48,48]{2,1,0:T(8,128)(2,1)} %param.5) | copy-start | bytes 207364
  15.9 2.1 %copy-start.2 = (bf16[15,3,1,48,8,128]{5,3,0,4,1,2:T(8,128)(2,1)}, bf16[15,3,1,48,8,128]{5,3,0,4,1,2:T(8,128)(2,1)S(1)}, u32[]{:S(2)}) copy-start(bf16[15,3,1,48,8,128]{5,3,0,4,1,2:T(8,128)(2,1)S(1)} %fusion.114) | copy-start | bytes 13271044
  18.0 5.0 %copy-start.5 = (bf16[15,48,48]{2,1,0:T(8,128)(2,1)S(1)}, bf16[15,48,48]{2,1,0:T(8,128)(2,1)}, u32[]{:S(2)}) copy-start(bf16[15,48,48]{2,1,0:T(8,128)(2,1)} %param.6) | copy-start | bytes 207364
  19.8 3.3 %collective-permute-start.2 = (bf16[2,3,1,48,8,7]{3,4,5,2,1,0:T(8,128)(2,1)S(1)}, bf16[2,3,1,48,8,7]{3,4,5,2,1,0:T(8,128)(2,1)S(1)}, u32[]{:S(2)}, u32[]{:S(2)}) collective-permute-start(bf16[2,3,1,48,8,7]{3,4,5,2,1,0:T(8,128)(2,1)S(1)} %copy.86), channel_id=1, source_target_pairs={{0,1},{1,2},{2,3},{3,4},{4,5},{5,6},{6,7},{8,9},{9,10},{10,11},{11... | collective-permute-start | bytes 96776 | tf_op jit(solution)/shard_map/ppermute | solution.py:15
  21.5 5.0 %collective-permute-start.3 = (bf16[2,3,1,48,8,7]{3,4,5,2,1,0:T(8,128)(2,1)S(1)}, bf16[2,3,1,48,8,7]{3,4,5,2,1,0:T(8,128)(2,1)S(1)}, u32[]{:S(2)}, u32[]{:S(2)}) collective-permute-start(bf16[2,3,1,48,8,7]{3,4,5,2,1,0:T(8,128)(2,1)S(1)} %copy.87), channel_id=1, source_target_pairs={{1,0},{2,1},{3,2},{4,3},{5,4},{6,5},{7,6},{9,8},{10,9},{11,10},{12... | collective-permute-start | bytes 96776 | tf_op jit(solution)/shard_map/ppermute | solution.py:17
  30.8 6.0 %slice-start = ((s8[4423680]{0:T(1024)(128)(4,1)}), s8[4194304]{0:T(1024)(128)(4,1)S(1)}, s32[]{:S(2)}) async-start(s8[4423680]{0:T(1024)(128)(4,1)} %bitcast.388), calls=%async_computation.2 | async-start | bytes 8388608
  32.9 3.8 %slice-start.1 = ((s8[4423680]{0:T(1024)(128)(4,1)}), s8[229376]{0:T(1024)(128)(4,1)S(1)}, s32[]{:S(2)}) async-start(s8[4423680]{0:T(1024)(128)(4,1)} %bitcast.388), calls=%async_computation.3 | async-start | bytes 458752
  33.3 2.0 %copy-start = (bf16[15,3,1,48,8,128]{5,3,4,1,2,0:T(8,128)(2,1)}, bf16[15,3,1,48,8,128]{5,3,4,1,2,0:T(8,128)(2,1)S(1)}, u32[]{:S(2)}) copy-start(bf16[15,3,1,48,8,128]{5,3,4,1,2,0:T(8,128)(2,1)S(1)} %get-tuple-element.29) | copy-start | bytes 13271044
  36.3 2.1 %copy-start.3 = (bf16[3,1,48,8,128]{4,3,2,1,0:T(8,128)(2,1)S(1)}, bf16[3,1,48,8,128]{4,3,2,1,0:T(8,128)(2,1)}, u32[]{:S(2)}) copy-start(bf16[3,1,48,8,128]{4,3,2,1,0:T(8,128)(2,1)} %param.7) | copy-start | bytes 884740
  42.1 20.6 %collective-permute-start.4 = (bf16[3,1,48,7,128]{4,2,3,0,1:T(8,128)(2,1)S(1)}, bf16[3,1,48,7,128]{4,2,3,0,1:T(8,128)(2,1)S(1)}, u32[]{:S(2)}, u32[]{:S(2)}) collective-permute-start(bf16[3,1,48,7,128]{4,2,3,0,1:T(8,128)(2,1)S(1)} %get-tuple-element.21), channel_id=1, source_target_pairs={{0,8},{8,16},{16,24},{24,32},{32,40},{40,48},{48,56},{56,64},{64,7... | collective-permute-start | bytes 774152 | tf_op jit(solution)/shard_map/ppermute | solution.py:15
  51.2 27.5 %all-to-all-start = ((f32[32,17,128]{2,1,0:T(8,128)}), f32[32,17,128]{2,1,0:T(8,128)S(1)}, u32[]{:S(2)}, u32[]{:S(2)}) async-start(f32[32,17,128]{2,1,0:T(8,128)} %reshape.60), calls=%async_computation | async-start | bytes 786432 | tf_op jit(solution)/shard_map/all_to_all | solution.py:63
  59.7 16.0 %collective-permute-start.5 = (bf16[3,1,48,7,128]{4,2,3,0,1:T(8,128)(2,1)S(1)}, bf16[3,1,48,7,128]{4,2,3,0,1:T(8,128)(2,1)S(1)}, u32[]{:S(2)}, u32[]{:S(2)}) collective-permute-start(bf16[3,1,48,7,128]{4,2,3,0,1:T(8,128)(2,1)S(1)} %get-tuple-element.20), channel_id=1, source_target_pairs={{8,0},{16,8},{24,16},{32,24},{40,32},{48,40},{56,48},{64,56},{72,6... | collective-permute-start | bytes 774152 | tf_op jit(solution)/shard_map/ppermute | solution.py:17
  78.7 1.8 %collective-permute-start.6 = (f32[17,128]{1,0:T(8,128)S(1)}, f32[17,128]{1,0:T(8,128)S(1)}, u32[]{:S(2)}, u32[]{:S(2)}) collective-permute-start(f32[17,128]{1,0:T(8,128)S(1)} %reduce_sum.9), channel_id=1, source_target_pairs={{0,1},{1,0},{2,3},{3,2},{4,5},{5,4},{6,7},{7,6},{8,9},{9,8},{10,11... | collective-permute-start | bytes 26120 | tf_op jit(solution)/shard_map/ppermute | solution.py:51
  80.5 5.0 %collective-permute-start.7 = (f32[17,128]{1,0:T(8,128)S(1)}, f32[17,128]{1,0:T(8,128)S(1)}, u32[]{:S(2)}, u32[]{:S(2)}) collective-permute-start(f32[17,128]{1,0:T(8,128)S(1)} %add.30), channel_id=1, source_target_pairs={{0,2},{1,3},{2,0},{3,1},{4,6},{5,7},{6,4},{7,5},{8,10},{9,11},{10,... | collective-permute-start | bytes 26120 | tf_op jit(solution)/shard_map/ppermute | solution.py:51
  85.5 5.5 %collective-permute-start.8 = (f32[17,128]{1,0:T(8,128)S(1)}, f32[17,128]{1,0:T(8,128)S(1)}, u32[]{:S(2)}, u32[]{:S(2)}) collective-permute-start(f32[17,128]{1,0:T(8,128)S(1)} %add.31), channel_id=1, source_target_pairs={{0,4},{1,5},{2,6},{3,7},{4,0},{5,1},{6,2},{7,3},{8,12},{9,13},{10,... | collective-permute-start | bytes 26120 | tf_op jit(solution)/shard_map/ppermute | solution.py:51
  91.8 22.1 %all-to-all-start.1 = ((f32[32,17,128]{2,1,0:T(8,128)}), f32[32,17,128]{2,1,0:T(8,128)S(1)}, u32[]{:S(2)}, u32[]{:S(2)}) async-start(f32[32,17,128]{2,1,0:T(8,128)} %broadcast_in_dim.2), calls=%async_computation.1 | async-start | bytes 786432 | tf_op jit(solution)/shard_map/all_to_all | solution.py:65

commit v5 on v4

--- a/solution.py
+++ b/solution.py
@@ -21,13 +21,37 @@
     return cells
 
 
-def conv_padded(padded, weight, dim):
+def conv_unfolded(padded, weight, dim):
     taps = weight.shape[0]
     length = padded.shape[dim] - taps + 1
     windows = jnp.stack(
         [lax.slice_in_dim(padded, tap, tap + length, axis=dim) for tap in range(taps)]
     )
     return jnp.einsum("kbzcxy,kco->bzoxy", windows, weight, preferred_element_type=jnp.float32)
+
+
+def conv_lax(padded, weight, dim):
+    b, z, c, x, y = padded.shape
+    cells = padded.reshape(b * z, c, x, y)
+    if dim == 4:
+        taps = weight.reshape((1,) + weight.shape)
+    else:
+        taps = weight.reshape((weight.shape[0], 1) + weight.shape[1:])
+    out = lax.conv_general_dilated(
+        cells,
+        taps,
+        (1, 1),
+        "VALID",
+        dimension_numbers=lax.ConvDimensionNumbers((0, 1, 2, 3), (3, 2, 0, 1), (0, 1, 2, 3)),
+        preferred_element_type=jnp.float32,
+    )
+    return out.reshape(b, z, out.shape[1], out.shape[2], out.shape[3])
+
+
+def conv_padded(padded, weight, dim, native=False):
+    if native:
+        return conv_lax(padded, weight, dim)
+    return conv_unfolded(padded, weight, dim)
 
 def flipped(weight):
     return jnp.transpose(jnp.flip(weight, 0), (0, 2, 1))
@@ -90,7 +114,7 @@
     wy_term = tap_products(act_pad, cotangent, taps, 4)
     grad_xpad = with_halo(pre_grad, (("gx", 3),), half)
     field_grad = (
-        cotangent.astype(jnp.float32) + conv_padded(grad_xpad, flipped(weight_x), 3)
+        cotangent.astype(jnp.float32) + conv_padded(grad_xpad, flipped(weight_x), 3, True)
     ).astype(jnp.bfloat16)
     wx_term = tap_products(field_pad, pre_grad, taps, 3)
     count = (

time: 117 us -> 106 us (0.906)
  other arithmetic: 12.2 us -> 2.07 us
  starting transfers between devices: 41.2 us -> 39.1 us
  local copies, waits for them, and re-layouts: 21.6 us -> 23.5 us
  waiting for transfers between devices: 26.5 us -> 24.7 us
  matrix products: 13.2 us -> 14.7 us
    unnamed x14 -> x1, other arithmetic: 9.6 us -> 0.01 us
    all_to_all x1, waiting for transfers between devices: 0.01 us -> 7.88 us  [global_sum(): mine = jnp.sum(lax.all_to_all(flat, scatter_axis, 0, 0, tiled=True), axis=0)]
    ppermute x3, waiting for transfers between devices: 12.3 us -> 5.32 us  [with_halo(): lax.ppermute(head, axis, [((i + 1) % count, i) for i in range(ends)])]
    conv_general_dilated x0 -> x1, matrix products: none -> 4.82 us  [conv_lax(): lax.conv_general_dilated(cells, taps, (1, 1), 'VALID', dimension_numbers=...]
    all_to_all x1, starting transfers between devices: 8.8 us -> 5.09 us  [global_sum(): lax.all_to_all(jnp.broadcast_to(mine[None], (devices, rows, lanes)), scat...]
    dot_general x4 -> x3, matrix products: 8.36 us -> 5.11 us  [conv_unfolded(): jnp.einsum('kbzcxy,kco->bzoxy', windows, weight, preferred_element_type=j...]
    all_to_all x1, starting transfers between devices: 8.49 us -> 10.9 us  [global_sum(): mine = jnp.sum(lax.all_to_all(flat, scatter_axis, 0, 0, tiled=True), axis=0)]
    reshape x0 -> x1, local copies, waits for them, and re-layouts: none -> 1.83 us  [conv_lax(): cells = padded.reshape(b * z, c, x, y)]
  transfers between devices with their start and end apart: 11 -> 11, of which waited for: 8 -> 6; matrix products, arithmetic and copies ran while one was open for 20% -> 15% of each run, Pallas kernels for 0% -> 0%
where the time goes in v5:
time: 106 us; the launch traced here: 105 us
  starting transfers between devices  39.1 us (37%)
  waiting for transfers between devices  24.7 us (23%)
  local copies, waits for them, and re-layouts  23.5 us (22%)
  matrix products  14.7 us (14%)
  other arithmetic  2.07 us (2%)
  between operations  1.27 us (1%)
    unnamed x66, local copies, waits for them, and re-layouts  14.2 us
    all_to_all x1, starting transfers between devices, global_sum(): mine = jnp.sum(lax.all_to_all(flat, scatter_axis, 0, 0, tiled=True), axis=0)  10.9 us
    ppermute x3, starting transfers between devices, tree_sum(): lax.ppermute(values, axis, [(i, i ^ step) for i in range(count)])  8.7 us
    ppermute x3, starting transfers between devices, with_halo(): lax.ppermute(tail, axis, [(i, (i + 1) % count) for i in range(ends)])  8.5 us
    all_to_all x1, waiting for transfers between devices, global_sum(): mine = jnp.sum(lax.all_to_all(flat, scatter_axis, 0, 0, tiled=True), axis=0)  7.88 us
    all_to_all x1, waiting for transfers between devices, global_sum(): lax.all_to_all(jnp.broadcast_to(mine[None], (devices, rows, lanes)), scat...  7.76 us
    ppermute x3, starting transfers between devices, with_halo(): lax.ppermute(head, axis, [((i + 1) % count, i) for i in range(ends)])  5.99 us
    ppermute x3, waiting for transfers between devices, with_halo(): lax.ppermute(head, axis, [((i + 1) % count, i) for i in range(ends)])  5.32 us
  transfers between devices with their start and end apart: 11, of which 6 were waited for; matrix products, arithmetic and copies ran while one was open for 15% of the time, Pallas kernels for 0%

profile of v5, /device:TPU:32, one launch (start us, length us, event | category | flops | bytes accessed | tf_op | source)
XLA Modules:
  0.0 105.5 jit_solution(4961783645541686039)
XLA Ops:
  0.6 1.2 %fusion.95 = (bf16[3,1,48,7,128]{4,3,2,1,0:T(8,128)(2,1)S(1)}, bf16[3,1,48,7,128]{4,3,2,1,0:T(8,128)(2,1)S(1)}) fusion(bf16[3,1,48,8,128]{4,3,2,1,0:T(8,128)(2,1)} %param.4), kind=kLoop, calls=%fused_computation.150 | loop fusion | bytes 1032192 | tf_op jit(solution)/shard_map/slice | solution.py:11
  1.9 3.8 %collective-permute-start = (bf16[3,1,48,7,128]{4,2,3,0,1:T(8,128)(2,1)S(1)}, bf16[3,1,48,7,128]{4,2,3,0,1:T(8,128)(2,1)S(1)}, u32[]{:S(2)}, u32[]{:S(2)}) collective-permute-start(bf16[3,1,48,7,128]{4,2,3,0,1:T(8,128)(2,1)S(1)} %copy.136), channel_id=1, source_target_pairs={{0,8},{8,16},{16,24},{24,32},{32,40},{40,48},{48,56},{56,64},{64,7... | collective-permute-start | bytes 774152 | tf_op jit(solution)/shard_map/ppermute | solution.py:15
  5.8 2.0 %collective-permute-start.1 = (bf16[3,1,48,7,128]{4,2,3,0,1:T(8,128)(2,1)S(1)}, bf16[3,1,48,7,128]{4,2,3,0,1:T(8,128)(2,1)S(1)}, u32[]{:S(2)}, u32[]{:S(2)}) collective-permute-start(bf16[3,1,48,7,128]{4,2,3,0,1:T(8,128)(2,1)S(1)} %copy.137), channel_id=1, source_target_pairs={{8,0},{16,8},{24,16},{32,24},{40,32},{48,40},{56,48},{64,56},{72,6... | collective-permute-start | bytes 774152 | tf_op jit(solution)/shard_map/ppermute | solution.py:17
  7.8 1.0 copy.138
  8.8 2.9 %collective-permute-done = bf16[3,1,48,7,128]{4,2,3,0,1:T(8,128)(2,1)S(1)} collective-permute-done((bf16[3,1,48,7,128]{4,2,3,0,1:T(8,128)(2,1)S(1)}, bf16[3,1,48,7,128]{4,2,3,0,1:T(8,128)(2,1)S(1)}, u32[]{:S(2)}, u32[]{:S(2)}) %collective-permute-start) | collective-permute-done | bytes 258080 | tf_op jit(solution)/shard_map/ppermute | solution.py:15
  11.7 1.1 %constant_dynamic-update-slice_fusion.3 = (bf16[3,1,48,15,128]{4,2,3,0,1:T(8,128)(2,1)S(1)}, bf16[3,1,48,15,128]{4,2,3,0,1:T(8,128)(2,1)S(1)}) fusion(bf16[3,1,48,8,128]{4,3,2,1,0:T(8,128)(2,1)} %param.4, bf16[3,1,48,15,128]{4,2,3,0,1:T(8,128)(2,1)S(1)} %constant_dynamic-update-slice_fusion.1), kind=kLoop, calls=%fused_computation.147 | loop fusion | bytes 884736
  13.2 2.3 %collective-permute-done.1 = bf16[3,1,48,7,128]{4,2,3,0,1:T(8,128)(2,1)S(1)} collective-permute-done((bf16[3,1,48,7,128]{4,2,3,0,1:T(8,128)(2,1)S(1)}, bf16[3,1,48,7,128]{4,2,3,0,1:T(8,128)(2,1)S(1)}, u32[]{:S(2)}, u32[]{:S(2)}) %collective-permute-start.1) | collective-permute-done | bytes 258080 | tf_op jit(solution)/shard_map/ppermute | solution.py:17
  15.9 2.1 %copy-done.2 = bf16[15,3,1,48,8,128]{5,3,0,4,1,2:T(8,128)(2,1)} copy-done((bf16[15,3,1,48,8,128]{5,3,0,4,1,2:T(8,128)(2,1)}, bf16[15,3,1,48,8,128]{5,3,0,4,1,2:T(8,128)(2,1)S(1)}, u32[]{:S(2)}) %copy-start.2) | copy-done | bytes 4423704
  18.0 0.9 fusion.27
  18.9 0.2 fusion.42
  19.1 0.2 slice_maximum_fusion
  19.4 0.4 copy.87
  19.8 1.3 %collective-permute-start.2 = (bf16[2,3,1,48,8,7]{3,4,5,2,1,0:T(8,128)(2,1)S(1)}, bf16[2,3,1,48,8,7]{3,4,5,2,1,0:T(8,128)(2,1)S(1)}, u32[]{:S(2)}, u32[]{:S(2)}) collective-permute-start(bf16[2,3,1,48,8,7]{3,4,5,2,1,0:T(8,128)(2,1)S(1)} %copy.87), channel_id=1, source_target_pairs={{0,1},{1,2},{2,3},{3,4},{4,5},{5,6},{6,7},{8,9},{9,10},{10,11},{11... | collective-permute-start | bytes 96776 | tf_op jit(solution)/shard_map/ppermute | solution.py:15
  21.1 0.4 copy.88
  21.5 1.5 %collective-permute-start.3 = (bf16[2,3,1,48,8,7]{3,4,5,2,1,0:T(8,128)(2,1)S(1)}, bf16[2,3,1,48,8,7]{3,4,5,2,1,0:T(8,128)(2,1)S(1)}, u32[]{:S(2)}, u32[]{:S(2)}) collective-permute-start(bf16[2,3,1,48,8,7]{3,4,5,2,1,0:T(8,128)(2,1)S(1)} %copy.88), channel_id=1, source_target_pairs={{1,0},{2,1},{3,2},{4,3},{5,4},{6,5},{7,6},{9,8},{10,9},{11,10},{12... | collective-permute-start | bytes 96776 | tf_op jit(solution)/shard_map/ppermute | solution.py:17
  23.0 0.4 copy.89
  23.4 3.0 %collective-permute-done.3 = bf16[2,3,1,48,8,7]{3,4,5,2,1,0:T(8,128)(2,1)S(1)} collective-permute-done((bf16[2,3,1,48,8,7]{3,4,5,2,1,0:T(8,128)(2,1)S(1)}, bf16[2,3,1,48,8,7]{3,4,5,2,1,0:T(8,128)(2,1)S(1)}, u32[]{:S(2)}, u32[]{:S(2)}) %collective-permute-start.3) | collective-permute-done | bytes 32288 | tf_op jit(solution)/shard_map/ppermute | solution.py:17
  26.5 0.4 copy.90
  26.9 0.7 pad_maximum_fusion
  27.8 0.2 fusion.71
  27.9 0.2 fusion.70
  28.1 0.2 fusion.69
  28.3 0.2 fusion.68
  28.5 0.2 fusion.67
  28.7 0.2 fusion.66
  28.9 0.2 fusion.65
  29.1 0.2 fusion.64
  29.3 0.2 fusion.63
  29.5 0.2 fusion.62
  29.7 0.2 fusion.61
  29.9 0.2 fusion.60
  30.1 0.2 fusion.59
  30.3 0.2 fusion.56
  30.5 0.2 fusion.55
  32.9 0.3 fusion.43
  33.2 2.0 %copy-done = bf16[15,3,1,48,8,128]{5,3,4,1,2,0:T(8,128)(2,1)} copy-done((bf16[15,3,1,48,8,128]{5,3,4,1,2,0:T(8,128)(2,1)}, bf16[15,3,1,48,8,128]{5,3,4,1,2,0:T(8,128)(2,1)S(1)}, u32[]{:S(2)}) %copy-start) | copy-done | bytes 4423704
  35.3 1.0 fusion.12
  36.3 0.4 fusion.33
  36.7 1.3 %fusion.21 = f32[15,48,48]{2,1,0:T(8,128)S(1)} fusion(bf16[15,3,1,48,8,128]{5,3,0,4,1,2:T(8,128)(2,1)S(1)} %bitcast.329, bf16[3,1,48,8,128]{4,2,3,0,1:T(8,128)(2,1)S(1)} %fusion.33), kind=kOutput, calls=%fused_computation.16 | convolution fusion | flops 212336640 | bytes 4856832 | tf_op jit(solution)/shard_map/kbzcxy,bzoxy->kco/dot_general | solution.py:65
  38.0 0.2 reshape.64
  38.3 3.5 %fusion.24 = f32[15,48,48]{2,1,0:T(8,128)S(1)} fusion(bf16[15,3,1,48,8,128]{5,3,4,1,2,0:T(8,128)(2,1)} %copy-done, bf16[3,48,8,128,1]{3,2,1,0,4:T(8,128)(2,1)S(1)} %bitcast.333), kind=kOutput, calls=%fused_computation.17 | convolution fusion | flops 212336640 | bytes 4856832 | tf_op jit(solution)/shard_map/kbzcxy,bzoxy->kco/dot_general | solution.py:65
  41.8 0.2 reshape.66
  42.1 0.8 reshape.67
  42.8 10.9 %all-to-all-start = ((f32[32,17,128]{2,1,0:T(8,128)}), f32[32,17,128]{2,1,0:T(8,128)S(1)}, u32[]{:S(2)}, u32[]{:S(2)}) async-start(f32[32,17,128]{2,1,0:T(8,128)} %reshape.67), calls=%async_computation | async-start | bytes 786432 | tf_op jit(solution)/shard_map/all_to_all | solution.py:87
  53.7 0.4 copy.93
  54.2 3.4 %collective-permute-start.4 = (bf16[3,1,48,7,128]{4,2,3,0,1:T(8,128)(2,1)S(1)}, bf16[3,1,48,7,128]{4,2,3,0,1:T(8,128)(2,1)S(1)}, u32[]{:S(2)}, u32[]{:S(2)}) collective-permute-start(bf16[3,1,48,7,128]{4,2,3,0,1:T(8,128)(2,1)S(1)} %get-tuple-element.20), channel_id=1, source_target_pairs={{0,8},{8,16},{16,24},{24,32},{32,40},{40,48},{48,56},{56,64},{64,7... | collective-permute-start | bytes 774152 | tf_op jit(solution)/shard_map/ppermute | solution.py:15
  57.6 2.5 %collective-permute-start.5 = (bf16[3,1,48,7,128]{4,2,3,0,1:T(8,128)(2,1)S(1)}, bf16[3,1,48,7,128]{4,2,3,0,1:T(8,128)(2,1)S(1)}, u32[]{:S(2)}, u32[]{:S(2)}) collective-permute-start(bf16[3,1,48,7,128]{4,2,3,0,1:T(8,128)(2,1)S(1)} %get-tuple-element.21), channel_id=1, source_target_pairs={{8,0},{16,8},{24,16},{32,24},{40,32},{48,40},{56,48},{64,56},{72,6... | collective-permute-start | bytes 774152 | tf_op jit(solution)/shard_map/ppermute | solution.py:17
  60.1 7.9 %all-to-all-done = f32[32,17,128]{2,1,0:T(8,128)S(1)} async-done(((f32[32,17,128]{2,1,0:T(8,128)}), f32[32,17,128]{2,1,0:T(8,128)S(1)}, u32[]{:S(2)}, u32[]{:S(2)}) %all-to-all-start) | async-done | bytes 278560 | tf_op jit(solution)/shard_map/all_to_all | solution.py:87
  68.0 2.6 %collective-permute-start.6 = (f32[17,128]{1,0:T(8,128)S(1)}, f32[17,128]{1,0:T(8,128)S(1)}, u32[]{:S(2)}, u32[]{:S(2)}) collective-permute-start(f32[17,128]{1,0:T(8,128)S(1)} %reduce_sum.9), channel_id=1, source_target_pairs={{0,1},{1,0},{2,3},{3,2},{4,5},{5,4},{6,7},{7,6},{8,9},{9,8},{10,11... | collective-permute-start | bytes 26120 | tf_op jit(solution)/shard_map/ppermute | solution.py:75
  70.6 3.2 %fusion.2 = f32[3,8,128,48,1]{2,3,1,0,4:T(8,128)S(1)} fusion(bf16[15,3,1,48,8,128]{5,3,4,1,2,0:T(8,128)(2,1)} %copy-done, bf16[15,48,48]{2,1,0:T(8,128)(2,1)S(1)} %copy-done.5), kind=kOutput, calls=%fused_computation.2 | convolution fusion | flops 212336640 | bytes 5082624 | tf_op jit(solution)/shard_map/kbzcxy,kco->bzoxy/dot_general | solution.py:30
  73.8 2.5 %collective-permute-start.7 = (f32[17,128]{1,0:T(8,128)S(1)}, f32[17,128]{1,0:T(8,128)S(1)}, u32[]{:S(2)}, u32[]{:S(2)}) collective-permute-start(f32[17,128]{1,0:T(8,128)S(1)} %add.30), channel_id=1, source_target_pairs={{0,2},{1,3},{2,0},{3,1},{4,6},{5,7},{6,4},{7,5},{8,10},{9,11},{10,... | collective-permute-start | bytes 26120 | tf_op jit(solution)/shard_map/ppermute | solution.py:75
  76.4 0.8 copy.102
  77.2 0.8 collective-permute-done.7
  78.0 3.6 %collective-permute-start.8 = (f32[17,128]{1,0:T(8,128)S(1)}, f32[17,128]{1,0:T(8,128)S(1)}, u32[]{:S(2)}, u32[]{:S(2)}) collective-permute-start(f32[17,128]{1,0:T(8,128)S(1)} %add.31), channel_id=1, source_target_pairs={{0,4},{1,5},{2,6},{3,7},{4,0},{5,1},{6,2},{7,3},{8,12},{9,13},{10,... | collective-permute-start | bytes 26120 | tf_op jit(solution)/shard_map/ppermute | solution.py:75
  81.7 1.8 %copy.96 = bf16[48,22,3,128]{0,3,2,1:T(8,128)(2,1)} copy(bf16[48,22,3,128]{3,0,1,2:T(8,128)(2,1)S(1)} %maximum_bitcast_fusion) | data formatting | bytes 1622016 | tf_op jit(solution)/shard_map/reshape | solution.py:35
  83.6 0.8 broadcast_in_dim.2
  84.3 5.1 %all-to-all-start.1 = ((f32[32,17,128]{2,1,0:T(8,128)}), f32[32,17,128]{2,1,0:T(8,128)S(1)}, u32[]{:S(2)}, u32[]{:S(2)}) async-start(f32[32,17,128]{2,1,0:T(8,128)} %broadcast_in_dim.2), calls=%async_computation.1 | async-start | bytes 786432 | tf_op jit(solution)/shard_map/all_to_all | solution.py:89
  89.4 4.8 %fusion.10 = f32[8,24,16,48]{3,1,2,0:T(8,128)S(1)} fusion(bf16[48,22,24,16]{0,3,2,1:T(8,128)(2,1)} %bitcast.332, bf16[15,48,48]{2,1,0:T(8,128)(2,1)S(1)} %rev.8), kind=kOutput, calls=%fused_computation.10 | convolution fusion | flops 212336640 | bytes 1469952 | tf_op jit(solution)/shard_map/conv_general_dilated | solution.py:40
  94.3 0.3 copy.99
  94.6 0.2 add_convert_fusion
  94.8 1.0 copy.103
  95.8 7.8 %all-to-all-done.1 = f32[32,17,128]{2,1,0:T(8,128)S(1)} async-done(((f32[32,17,128]{2,1,0:T(8,128)}), f32[32,17,128]{2,1,0:T(8,128)S(1)}, u32[]{:S(2)}, u32[]{:S(2)}) %all-to-all-start.1) | async-done | bytes 278560 | tf_op jit(solution)/shard_map/all_to_all | solution.py:89
  103.6 0.9 reshape.69
  104.6 0.9 reshape.70
  (65 shorter events, 3.4 us)
Async XLA Ops:
  0.6 12.5 %copy-start.1 = (bf16[3,1,48,8,128]{4,3,2,1,0:T(8,128)(2,1)S(1)}, bf16[3,1,48,8,128]{4,3,2,1,0:T(8,128)(2,1)}, u32[]{:S(2)}) copy-start(bf16[3,1,48,8,128]{4,3,2,1,0:T(8,128)(2,1)} %param.4) | copy-start | bytes 884740
  1.9 9.9 %collective-permute-start = (bf16[3,1,48,7,128]{4,2,3,0,1:T(8,128)(2,1)S(1)}, bf16[3,1,48,7,128]{4,2,3,0,1:T(8,128)(2,1)S(1)}, u32[]{:S(2)}, u32[]{:S(2)}) collective-permute-start(bf16[3,1,48,7,128]{4,2,3,0,1:T(8,128)(2,1)S(1)} %copy.136), channel_id=1, source_target_pairs={{0,8},{8,16},{16,24},{24,32},{32,40},{40,48},{48,56},{56,64},{64,7... | collective-permute-start | bytes 774152 | tf_op jit(solution)/shard_map/ppermute | solution.py:15
  5.8 9.8 %collective-permute-start.1 = (bf16[3,1,48,7,128]{4,2,3,0,1:T(8,128)(2,1)S(1)}, bf16[3,1,48,7,128]{4,2,3,0,1:T(8,128)(2,1)S(1)}, u32[]{:S(2)}, u32[]{:S(2)}) collective-permute-start(bf16[3,1,48,7,128]{4,2,3,0,1:T(8,128)(2,1)S(1)} %copy.137), channel_id=1, source_target_pairs={{8,0},{16,8},{24,16},{32,24},{40,32},{48,40},{56,48},{64,56},{72,6... | collective-permute-start | bytes 774152 | tf_op jit(solution)/shard_map/ppermute | solution.py:17
  12.9 5.1 %copy-start.4 = (bf16[15,48,48]{2,1,0:T(8,128)(2,1)S(1)}, bf16[15,48,48]{2,1,0:T(8,128)(2,1)}, u32[]{:S(2)}) copy-start(bf16[15,48,48]{2,1,0:T(8,128)(2,1)} %param.5) | copy-start | bytes 207364
  15.9 2.1 %copy-start.2 = (bf16[15,3,1,48,8,128]{5,3,0,4,1,2:T(8,128)(2,1)}, bf16[15,3,1,48,8,128]{5,3,0,4,1,2:T(8,128)(2,1)S(1)}, u32[]{:S(2)}) copy-start(bf16[15,3,1,48,8,128]{5,3,0,4,1,2:T(8,128)(2,1)S(1)} %fusion.73) | copy-start | bytes 13271044
  18.0 5.0 %copy-start.5 = (bf16[15,48,48]{2,1,0:T(8,128)(2,1)S(1)}, bf16[15,48,48]{2,1,0:T(8,128)(2,1)}, u32[]{:S(2)}) copy-start(bf16[15,48,48]{2,1,0:T(8,128)(2,1)} %param.6) | copy-start | bytes 207364
  19.8 3.2 %collective-permute-start.2 = (bf16[2,3,1,48,8,7]{3,4,5,2,1,0:T(8,128)(2,1)S(1)}, bf16[2,3,1,48,8,7]{3,4,5,2,1,0:T(8,128)(2,1)S(1)}, u32[]{:S(2)}, u32[]{:S(2)}) collective-permute-start(bf16[2,3,1,48,8,7]{3,4,5,2,1,0:T(8,128)(2,1)S(1)} %copy.87), channel_id=1, source_target_pairs={{0,1},{1,2},{2,3},{3,4},{4,5},{5,6},{6,7},{8,9},{9,10},{10,11},{11... | collective-permute-start | bytes 96776 | tf_op jit(solution)/shard_map/ppermute | solution.py:15
  21.5 5.0 %collective-permute-start.3 = (bf16[2,3,1,48,8,7]{3,4,5,2,1,0:T(8,128)(2,1)S(1)}, bf16[2,3,1,48,8,7]{3,4,5,2,1,0:T(8,128)(2,1)S(1)}, u32[]{:S(2)}, u32[]{:S(2)}) collective-permute-start(bf16[2,3,1,48,8,7]{3,4,5,2,1,0:T(8,128)(2,1)S(1)} %copy.88), channel_id=1, source_target_pairs={{1,0},{2,1},{3,2},{4,3},{5,4},{6,5},{7,6},{9,8},{10,9},{11,10},{12... | collective-permute-start | bytes 96776 | tf_op jit(solution)/shard_map/ppermute | solution.py:17
  30.7 6.0 %slice-start = ((s8[4423680]{0:T(1024)(128)(4,1)}), s8[4194304]{0:T(1024)(128)(4,1)S(1)}, s32[]{:S(2)}) async-start(s8[4423680]{0:T(1024)(128)(4,1)} %bitcast.328), calls=%async_computation.2 | async-start | bytes 8388608
  32.9 3.8 %slice-start.1 = ((s8[4423680]{0:T(1024)(128)(4,1)}), s8[229376]{0:T(1024)(128)(4,1)S(1)}, s32[]{:S(2)}) async-start(s8[4423680]{0:T(1024)(128)(4,1)} %bitcast.328), calls=%async_computation.3 | async-start | bytes 458752
  33.2 2.0 %copy-start = (bf16[15,3,1,48,8,128]{5,3,4,1,2,0:T(8,128)(2,1)}, bf16[15,3,1,48,8,128]{5,3,4,1,2,0:T(8,128)(2,1)S(1)}, u32[]{:S(2)}) copy-start(bf16[15,3,1,48,8,128]{5,3,4,1,2,0:T(8,128)(2,1)S(1)} %get-tuple-element.29) | copy-start | bytes 13271044
  36.3 2.0 %copy-start.3 = (bf16[3,1,48,8,128]{4,3,2,1,0:T(8,128)(2,1)S(1)}, bf16[3,1,48,8,128]{4,3,2,1,0:T(8,128)(2,1)}, u32[]{:S(2)}) copy-start(bf16[3,1,48,8,128]{4,3,2,1,0:T(8,128)(2,1)} %param.7) | copy-start | bytes 884740
  42.8 25.1 %all-to-all-start = ((f32[32,17,128]{2,1,0:T(8,128)}), f32[32,17,128]{2,1,0:T(8,128)S(1)}, u32[]{:S(2)}, u32[]{:S(2)}) async-start(f32[32,17,128]{2,1,0:T(8,128)} %reshape.67), calls=%async_computation | async-start | bytes 786432 | tf_op jit(solution)/shard_map/all_to_all | solution.py:87
  54.2 27.4 %collective-permute-start.4 = (bf16[3,1,48,7,128]{4,2,3,0,1:T(8,128)(2,1)S(1)}, bf16[3,1,48,7,128]{4,2,3,0,1:T(8,128)(2,1)S(1)}, u32[]{:S(2)}, u32[]{:S(2)}) collective-permute-start(bf16[3,1,48,7,128]{4,2,3,0,1:T(8,128)(2,1)S(1)} %get-tuple-element.20), channel_id=1, source_target_pairs={{0,8},{8,16},{16,24},{24,32},{32,40},{40,48},{48,56},{56,64},{64,7... | collective-permute-start | bytes 774152 | tf_op jit(solution)/shard_map/ppermute | solution.py:15
  57.6 24.0 %collective-permute-start.5 = (bf16[3,1,48,7,128]{4,2,3,0,1:T(8,128)(2,1)S(1)}, bf16[3,1,48,7,128]{4,2,3,0,1:T(8,128)(2,1)S(1)}, u32[]{:S(2)}, u32[]{:S(2)}) collective-permute-start(bf16[3,1,48,7,128]{4,2,3,0,1:T(8,128)(2,1)S(1)} %get-tuple-element.21), channel_id=1, source_target_pairs={{8,0},{16,8},{24,16},{32,24},{40,32},{48,40},{56,48},{64,56},{72,6... | collective-permute-start | bytes 774152 | tf_op jit(solution)/shard_map/ppermute | solution.py:17
  68.0 5.8 %collective-permute-start.6 = (f32[17,128]{1,0:T(8,128)S(1)}, f32[17,128]{1,0:T(8,128)S(1)}, u32[]{:S(2)}, u32[]{:S(2)}) collective-permute-start(f32[17,128]{1,0:T(8,128)S(1)} %reduce_sum.9), channel_id=1, source_target_pairs={{0,1},{1,0},{2,3},{3,2},{4,5},{5,4},{6,7},{7,6},{8,9},{9,8},{10,11... | collective-permute-start | bytes 26120 | tf_op jit(solution)/shard_map/ppermute | solution.py:75
  73.8 4.2 %collective-permute-start.7 = (f32[17,128]{1,0:T(8,128)S(1)}, f32[17,128]{1,0:T(8,128)S(1)}, u32[]{:S(2)}, u32[]{:S(2)}) collective-permute-start(f32[17,128]{1,0:T(8,128)S(1)} %add.30), channel_id=1, source_target_pairs={{0,2},{1,3},{2,0},{3,1},{4,6},{5,7},{6,4},{7,5},{8,10},{9,11},{10,... | collective-permute-start | bytes 26120 | tf_op jit(solution)/shard_map/ppermute | solution.py:75
  78.0 5.5 %collective-permute-start.8 = (f32[17,128]{1,0:T(8,128)S(1)}, f32[17,128]{1,0:T(8,128)S(1)}, u32[]{:S(2)}, u32[]{:S(2)}) collective-permute-start(f32[17,128]{1,0:T(8,128)S(1)} %add.31), channel_id=1, source_target_pairs={{0,4},{1,5},{2,6},{3,7},{4,0},{5,1},{6,2},{7,3},{8,12},{9,13},{10,... | collective-permute-start | bytes 26120 | tf_op jit(solution)/shard_map/ppermute | solution.py:75
  84.3 19.2 %all-to-all-start.1 = ((f32[32,17,128]{2,1,0:T(8,128)}), f32[32,17,128]{2,1,0:T(8,128)S(1)}, u32[]{:S(2)}, u32[]{:S(2)}) async-start(f32[32,17,128]{2,1,0:T(8,128)} %broadcast_in_dim.2), calls=%async_computation.1 | async-start | bytes 786432 | tf_op jit(solution)/shard_map/all_to_all | solution.py:89

commit v6 on v5

--- a/solution.py
+++ b/solution.py
@@ -108,10 +108,18 @@
     act_pad = paired[0]
     grad_pad = paired[1]
     output = (field.astype(jnp.float32) + conv_padded(act_pad, weight_y, 4)).astype(jnp.bfloat16)
-    act_grad = conv_padded(grad_pad, flipped(weight_y), 4)
+    length = field.shape[4]
+    grad_windows = jnp.stack(
+        [lax.slice_in_dim(grad_pad, tap, tap + length, axis=4) for tap in range(taps)]
+    )
+    act_grad = jnp.einsum(
+        "kbzcxy,kco->bzoxy", grad_windows, flipped(weight_y), preferred_element_type=jnp.float32
+    )
     _, pull = jax.vjp(jax.nn.gelu, pre.astype(jnp.float32))
     pre_grad = pull(act_grad)[0].astype(jnp.bfloat16)
-    wy_term = tap_products(act_pad, cotangent, taps, 4)
+    wy_term = jnp.flip(
+        jnp.einsum("kbzoxy,bzcxy->kco", grad_windows, act, preferred_element_type=jnp.float32), 0
+    )
     grad_xpad = with_halo(pre_grad, (("gx", 3),), half)
     field_grad = (
         cotangent.astype(jnp.float32) + conv_padded(grad_xpad, flipped(weight_x), 3, True)

time: 106 us -> 105 us (level)
    dot_general x0 -> x2, matrix products: none -> 3.57 us  [the longest x1 2.54 us: per_device(): jnp.einsum('kbzoxy,bzcxy->kco', grad_windows, act, preferred_element_type...]
    dot_general x2 -> x1, matrix products: 4.81 us -> 1.28 us  [tap_products(): jnp.einsum('kbzcxy,bzoxy->kco', windows, grads, preferred_element_type=jn...]
    dot_general x3 -> x2, matrix products: 5.11 us -> 4.11 us  [conv_unfolded(): jnp.einsum('kbzcxy,kco->bzoxy', windows, weight, preferred_element_type=j...]
where the time goes in v6:
time: 105 us
  starting transfers between devices  39.1 us (37%)
  waiting for transfers between devices  24.7 us (24%)
  local copies, waits for them, and re-layouts  23.8 us (23%)
  matrix products  13.8 us (13%)
  other arithmetic  2.07 us (2%)
  between operations  1.32 us (1%)
    unnamed x66, local copies, waits for them, and re-layouts  14.4 us
    all_to_all x1, starting transfers between devices, global_sum(): mine = jnp.sum(lax.all_to_all(flat, scatter_axis, 0, 0, tiled=True), axis=0)  10.9 us
    ppermute x3, starting transfers between devices, tree_sum(): lax.ppermute(values, axis, [(i, i ^ step) for i in range(count)])  8.71 us
    ppermute x3, starting transfers between devices, with_halo(): lax.ppermute(tail, axis, [(i, (i + 1) % count) for i in range(ends)])  8.5 us
    all_to_all x1, waiting for transfers between devices, global_sum(): mine = jnp.sum(lax.all_to_all(flat, scatter_axis, 0, 0, tiled=True), axis=0)  7.87 us
    all_to_all x1, waiting for transfers between devices, global_sum(): lax.all_to_all(jnp.broadcast_to(mine[None], (devices, rows, lanes)), scat...  7.78 us
    ppermute x3, starting transfers between devices, with_halo(): lax.ppermute(head, axis, [((i + 1) % count, i) for i in range(ends)])  5.99 us
    ppermute x3, waiting for transfers between devices, with_halo(): lax.ppermute(head, axis, [((i + 1) % count, i) for i in range(ends)])  5.32 us
  transfers between devices with their start and end apart: 11, of which 6 were waited for; matrix products, arithmetic and copies ran while one was open for 15% of the time, Pallas kernels for 0%

profile of v6, /device:TPU:32, one launch (start us, length us, event | category | flops | bytes accessed | tf_op | source)
XLA Modules:
  0.0 104.8 jit_solution(2639848055728068783)
XLA Ops:
  0.6 1.2 %fusion.91 = (bf16[3,1,48,7,128]{4,3,2,1,0:T(8,128)(2,1)S(1)}, bf16[3,1,48,7,128]{4,3,2,1,0:T(8,128)(2,1)S(1)}) fusion(bf16[3,1,48,8,128]{4,3,2,1,0:T(8,128)(2,1)} %param.4), kind=kLoop, calls=%fused_computation.148 | loop fusion | bytes 1032192 | tf_op jit(solution)/shard_map/slice | solution.py:11
  1.9 3.8 %collective-permute-start = (bf16[3,1,48,7,128]{4,2,3,0,1:T(8,128)(2,1)S(1)}, bf16[3,1,48,7,128]{4,2,3,0,1:T(8,128)(2,1)S(1)}, u32[]{:S(2)}, u32[]{:S(2)}) collective-permute-start(bf16[3,1,48,7,128]{4,2,3,0,1:T(8,128)(2,1)S(1)} %copy.127), channel_id=1, source_target_pairs={{0,8},{8,16},{16,24},{24,32},{32,40},{40,48},{48,56},{56,64},{64,7... | collective-permute-start | bytes 774152 | tf_op jit(solution)/shard_map/ppermute | solution.py:15
  5.8 2.0 %collective-permute-start.1 = (bf16[3,1,48,7,128]{4,2,3,0,1:T(8,128)(2,1)S(1)}, bf16[3,1,48,7,128]{4,2,3,0,1:T(8,128)(2,1)S(1)}, u32[]{:S(2)}, u32[]{:S(2)}) collective-permute-start(bf16[3,1,48,7,128]{4,2,3,0,1:T(8,128)(2,1)S(1)} %copy.128), channel_id=1, source_target_pairs={{8,0},{16,8},{24,16},{32,24},{40,32},{48,40},{56,48},{64,56},{72,6... | collective-permute-start | bytes 774152 | tf_op jit(solution)/shard_map/ppermute | solution.py:17
  7.8 1.0 copy.129
  8.8 2.9 %collective-permute-done = bf16[3,1,48,7,128]{4,2,3,0,1:T(8,128)(2,1)S(1)} collective-permute-done((bf16[3,1,48,7,128]{4,2,3,0,1:T(8,128)(2,1)S(1)}, bf16[3,1,48,7,128]{4,2,3,0,1:T(8,128)(2,1)S(1)}, u32[]{:S(2)}, u32[]{:S(2)}) %collective-permute-start) | collective-permute-done | bytes 258080 | tf_op jit(solution)/shard_map/ppermute | solution.py:15
  11.7 1.1 %constant_dynamic-update-slice_fusion.3 = (bf16[3,1,48,15,128]{4,2,3,0,1:T(8,128)(2,1)S(1)}, bf16[3,1,48,15,128]{4,2,3,0,1:T(8,128)(2,1)S(1)}) fusion(bf16[3,1,48,8,128]{4,3,2,1,0:T(8,128)(2,1)} %param.4, bf16[3,1,48,15,128]{4,2,3,0,1:T(8,128)(2,1)S(1)} %constant_dynamic-update-slice_fusion.1), kind=kLoop, calls=%fused_computation.143 | loop fusion | bytes 884736
  13.2 2.3 %collective-permute-done.1 = bf16[3,1,48,7,128]{4,2,3,0,1:T(8,128)(2,1)S(1)} collective-permute-done((bf16[3,1,48,7,128]{4,2,3,0,1:T(8,128)(2,1)S(1)}, bf16[3,1,48,7,128]{4,2,3,0,1:T(8,128)(2,1)S(1)}, u32[]{:S(2)}, u32[]{:S(2)}) %collective-permute-start.1) | collective-permute-done | bytes 258080 | tf_op jit(solution)/shard_map/ppermute | solution.py:17
  15.9 2.1 %copy-done.2 = bf16[15,3,1,48,8,128]{5,3,0,4,1,2:T(8,128)(2,1)} copy-done((bf16[15,3,1,48,8,128]{5,3,0,4,1,2:T(8,128)(2,1)}, bf16[15,3,1,48,8,128]{5,3,0,4,1,2:T(8,128)(2,1)S(1)}, u32[]{:S(2)}) %copy-start.2) | copy-done | bytes 4423704
  18.0 0.9 fusion.22
  18.9 0.2 fusion.89
  19.1 0.2 slice_maximum_fusion
  19.4 0.4 copy.85
  19.8 1.3 %collective-permute-start.2 = (bf16[2,3,1,48,8,7]{3,4,5,2,1,0:T(8,128)(2,1)S(1)}, bf16[2,3,1,48,8,7]{3,4,5,2,1,0:T(8,128)(2,1)S(1)}, u32[]{:S(2)}, u32[]{:S(2)}) collective-permute-start(bf16[2,3,1,48,8,7]{3,4,5,2,1,0:T(8,128)(2,1)S(1)} %copy.85), channel_id=1, source_target_pairs={{0,1},{1,2},{2,3},{3,4},{4,5},{5,6},{6,7},{8,9},{9,10},{10,11},{11... | collective-permute-start | bytes 96776 | tf_op jit(solution)/shard_map/ppermute | solution.py:15
  21.1 0.4 copy.86
  21.5 1.5 %collective-permute-start.3 = (bf16[2,3,1,48,8,7]{3,4,5,2,1,0:T(8,128)(2,1)S(1)}, bf16[2,3,1,48,8,7]{3,4,5,2,1,0:T(8,128)(2,1)S(1)}, u32[]{:S(2)}, u32[]{:S(2)}) collective-permute-start(bf16[2,3,1,48,8,7]{3,4,5,2,1,0:T(8,128)(2,1)S(1)} %copy.86), channel_id=1, source_target_pairs={{1,0},{2,1},{3,2},{4,3},{5,4},{6,5},{7,6},{9,8},{10,9},{11,10},{12... | collective-permute-start | bytes 96776 | tf_op jit(solution)/shard_map/ppermute | solution.py:17
  23.0 0.4 copy.87
  23.4 3.0 %collective-permute-done.3 = bf16[2,3,1,48,8,7]{3,4,5,2,1,0:T(8,128)(2,1)S(1)} collective-permute-done((bf16[2,3,1,48,8,7]{3,4,5,2,1,0:T(8,128)(2,1)S(1)}, bf16[2,3,1,48,8,7]{3,4,5,2,1,0:T(8,128)(2,1)S(1)}, u32[]{:S(2)}, u32[]{:S(2)}) %collective-permute-start.3) | collective-permute-done | bytes 32288 | tf_op jit(solution)/shard_map/ppermute | solution.py:17
  26.5 0.4 copy.88
  26.9 0.7 pad_maximum_fusion
  27.8 0.2 fusion.65
  27.9 0.2 fusion.64
  30.3 0.2 fusion.50
  30.5 0.2 fusion.49
  30.7 0.2 fusion.48
  30.9 0.2 fusion.47
  31.1 0.2 fusion.46
  31.3 0.2 fusion.45
  31.5 0.2 fusion.44
  31.7 0.2 fusion.43
  31.9 0.2 fusion.42
  32.1 0.2 fusion.41
  32.3 0.2 fusion.40
  32.6 0.2 fusion.39
  32.8 0.2 fusion.38
  33.0 0.3 fusion.37
  33.3 2.2 %copy-done = bf16[15,3,1,48,8,128]{5,3,4,1,2,0:T(8,128)(2,1)} copy-done((bf16[15,3,1,48,8,128]{5,3,4,1,2,0:T(8,128)(2,1)}, bf16[15,3,1,48,8,128]{5,3,4,1,2,0:T(8,128)(2,1)S(1)}, u32[]{:S(2)}) %copy-start) | copy-done | bytes 4423704
  35.6 2.5 %convolution_bitcast_fusion = f32[15,48,48]{2,1,0:T(8,128)S(1)} fusion(bf16[15,3,1,48,8,128]{5,3,4,1,2,0:T(8,128)(2,1)S(1)} %get-tuple-element.28, bf16[3,1,48,8,128]{4,2,3,0,1:T(8,128)(2,1)S(1)} %fusion.22), kind=kOutput, calls=%fused_computation.15 | convolution fusion | flops 213811200 | bytes 4856832 | tf_op jit(solution)/shard_map/kbzoxy,bzcxy->kco/dot_general | solution.py:121
  38.1 1.0 fusion.10
  39.1 0.4 fusion.28
  39.6 1.3 %fusion.19 = f32[15,48,48]{2,1,0:T(8,128)S(1)} fusion(bf16[15,3,1,48,8,128]{5,3,0,4,1,2:T(8,128)(2,1)S(1)} %bitcast.331, bf16[3,1,48,8,128]{4,2,3,0,1:T(8,128)(2,1)S(1)} %fusion.28), kind=kOutput, calls=%fused_computation.14 | convolution fusion | flops 212336640 | bytes 4856832 | tf_op jit(solution)/shard_map/kbzcxy,bzoxy->kco/dot_general | solution.py:65
  40.9 0.2 reshape.64
  41.2 0.2 reshape.66
  41.4 0.8 reshape.67
  42.2 10.9 %all-to-all-start = ((f32[32,17,128]{2,1,0:T(8,128)}), f32[32,17,128]{2,1,0:T(8,128)S(1)}, u32[]{:S(2)}, u32[]{:S(2)}) async-start(f32[32,17,128]{2,1,0:T(8,128)} %reshape.67), calls=%async_computation | async-start | bytes 786432 | tf_op jit(solution)/shard_map/all_to_all | solution.py:87
  53.1 0.4 copy.91
  53.6 3.4 %collective-permute-start.4 = (bf16[3,1,48,7,128]{4,2,3,0,1:T(8,128)(2,1)S(1)}, bf16[3,1,48,7,128]{4,2,3,0,1:T(8,128)(2,1)S(1)}, u32[]{:S(2)}, u32[]{:S(2)}) collective-permute-start(bf16[3,1,48,7,128]{4,2,3,0,1:T(8,128)(2,1)S(1)} %get-tuple-element.20), channel_id=1, source_target_pairs={{0,8},{8,16},{16,24},{24,32},{32,40},{40,48},{48,56},{56,64},{64,7... | collective-permute-start | bytes 774152 | tf_op jit(solution)/shard_map/ppermute | solution.py:15
  57.0 2.5 %collective-permute-start.5 = (bf16[3,1,48,7,128]{4,2,3,0,1:T(8,128)(2,1)S(1)}, bf16[3,1,48,7,128]{4,2,3,0,1:T(8,128)(2,1)S(1)}, u32[]{:S(2)}, u32[]{:S(2)}) collective-permute-start(bf16[3,1,48,7,128]{4,2,3,0,1:T(8,128)(2,1)S(1)} %get-tuple-element.21), channel_id=1, source_target_pairs={{8,0},{16,8},{24,16},{32,24},{40,32},{48,40},{56,48},{64,56},{72,6... | collective-permute-start | bytes 774152 | tf_op jit(solution)/shard_map/ppermute | solution.py:17
  59.5 7.9 %all-to-all-done = f32[32,17,128]{2,1,0:T(8,128)S(1)} async-done(((f32[32,17,128]{2,1,0:T(8,128)}), f32[32,17,128]{2,1,0:T(8,128)S(1)}, u32[]{:S(2)}, u32[]{:S(2)}) %all-to-all-start) | async-done | bytes 278560 | tf_op jit(solution)/shard_map/all_to_all | solution.py:87
  67.4 2.6 %collective-permute-start.6 = (f32[17,128]{1,0:T(8,128)S(1)}, f32[17,128]{1,0:T(8,128)S(1)}, u32[]{:S(2)}, u32[]{:S(2)}) collective-permute-start(f32[17,128]{1,0:T(8,128)S(1)} %reduce_sum.9), channel_id=1, source_target_pairs={{0,1},{1,0},{2,3},{3,2},{4,5},{5,4},{6,7},{7,6},{8,9},{9,8},{10,11... | collective-permute-start | bytes 26120 | tf_op jit(solution)/shard_map/ppermute | solution.py:75
  70.0 3.2 %fusion = f32[3,8,128,48,1]{2,3,1,0,4:T(8,128)S(1)} fusion(bf16[15,3,1,48,8,128]{5,3,4,1,2,0:T(8,128)(2,1)} %copy-done, bf16[15,48,48]{2,1,0:T(8,128)(2,1)S(1)} %copy-done.5), kind=kOutput, calls=%fused_computation | convolution fusion | flops 212336640 | bytes 5082624 | tf_op jit(solution)/shard_map/kbzcxy,kco->bzoxy/dot_general | solution.py:30
  73.2 2.5 %collective-permute-start.7 = (f32[17,128]{1,0:T(8,128)S(1)}, f32[17,128]{1,0:T(8,128)S(1)}, u32[]{:S(2)}, u32[]{:S(2)}) collective-permute-start(f32[17,128]{1,0:T(8,128)S(1)} %add.30), channel_id=1, source_target_pairs={{0,2},{1,3},{2,0},{3,1},{4,6},{5,7},{6,4},{7,5},{8,10},{9,11},{10,... | collective-permute-start | bytes 26120 | tf_op jit(solution)/shard_map/ppermute | solution.py:75
  75.8 0.8 copy.99
  76.5 0.8 collective-permute-done.7
  77.4 3.6 %collective-permute-start.8 = (f32[17,128]{1,0:T(8,128)S(1)}, f32[17,128]{1,0:T(8,128)S(1)}, u32[]{:S(2)}, u32[]{:S(2)}) collective-permute-start(f32[17,128]{1,0:T(8,128)S(1)} %add.31), channel_id=1, source_target_pairs={{0,4},{1,5},{2,6},{3,7},{4,0},{5,1},{6,2},{7,3},{8,12},{9,13},{10,... | collective-permute-start | bytes 26120 | tf_op jit(solution)/shard_map/ppermute | solution.py:75
  81.1 1.8 %copy.94 = bf16[48,22,3,128]{0,3,2,1:T(8,128)(2,1)} copy(bf16[48,22,3,128]{3,0,1,2:T(8,128)(2,1)S(1)} %maximum_bitcast_fusion) | data formatting | bytes 1622016 | tf_op jit(solution)/shard_map/reshape | solution.py:35
  82.9 0.8 broadcast_in_dim.2
  83.7 5.1 %all-to-all-start.1 = ((f32[32,17,128]{2,1,0:T(8,128)}), f32[32,17,128]{2,1,0:T(8,128)S(1)}, u32[]{:S(2)}, u32[]{:S(2)}) async-start(f32[32,17,128]{2,1,0:T(8,128)} %broadcast_in_dim.2), calls=%async_computation.1 | async-start | bytes 786432 | tf_op jit(solution)/shard_map/all_to_all | solution.py:89
  88.8 4.8 %fusion.8 = f32[8,24,16,48]{3,1,2,0:T(8,128)S(1)} fusion(bf16[48,22,24,16]{0,3,2,1:T(8,128)(2,1)} %bitcast.334, bf16[15,48,48]{2,1,0:T(8,128)(2,1)S(1)} %rev.12), kind=kOutput, calls=%fused_computation.8 | convolution fusion | flops 212336640 | bytes 1469952 | tf_op jit(solution)/shard_map/conv_general_dilated | solution.py:40
  93.6 0.3 copy.97
  93.9 0.2 add_convert_fusion
  94.2 1.0 copy.100
  95.2 7.8 %all-to-all-done.1 = f32[32,17,128]{2,1,0:T(8,128)S(1)} async-done(((f32[32,17,128]{2,1,0:T(8,128)}), f32[32,17,128]{2,1,0:T(8,128)S(1)}, u32[]{:S(2)}, u32[]{:S(2)}) %all-to-all-start.1) | async-done | bytes 278560 | tf_op jit(solution)/shard_map/all_to_all | solution.py:89
  103.0 0.9 reshape.69
  103.9 0.9 reshape.70
  (66 shorter events, 3.5 us)
Async XLA Ops:
  0.6 12.5 %copy-start.1 = (bf16[3,1,48,8,128]{4,3,2,1,0:T(8,128)(2,1)S(1)}, bf16[3,1,48,8,128]{4,3,2,1,0:T(8,128)(2,1)}, u32[]{:S(2)}) copy-start(bf16[3,1,48,8,128]{4,3,2,1,0:T(8,128)(2,1)} %param.4) | copy-start | bytes 884740
  1.9 9.9 %collective-permute-start = (bf16[3,1,48,7,128]{4,2,3,0,1:T(8,128)(2,1)S(1)}, bf16[3,1,48,7,128]{4,2,3,0,1:T(8,128)(2,1)S(1)}, u32[]{:S(2)}, u32[]{:S(2)}) collective-permute-start(bf16[3,1,48,7,128]{4,2,3,0,1:T(8,128)(2,1)S(1)} %copy.127), channel_id=1, source_target_pairs={{0,8},{8,16},{16,24},{24,32},{32,40},{40,48},{48,56},{56,64},{64,7... | collective-permute-start | bytes 774152 | tf_op jit(solution)/shard_map/ppermute | solution.py:15
  5.8 9.8 %collective-permute-start.1 = (bf16[3,1,48,7,128]{4,2,3,0,1:T(8,128)(2,1)S(1)}, bf16[3,1,48,7,128]{4,2,3,0,1:T(8,128)(2,1)S(1)}, u32[]{:S(2)}, u32[]{:S(2)}) collective-permute-start(bf16[3,1,48,7,128]{4,2,3,0,1:T(8,128)(2,1)S(1)} %copy.128), channel_id=1, source_target_pairs={{8,0},{16,8},{24,16},{32,24},{40,32},{48,40},{56,48},{64,56},{72,6... | collective-permute-start | bytes 774152 | tf_op jit(solution)/shard_map/ppermute | solution.py:17
  12.9 5.1 %copy-start.4 = (bf16[15,48,48]{2,1,0:T(8,128)(2,1)S(1)}, bf16[15,48,48]{2,1,0:T(8,128)(2,1)}, u32[]{:S(2)}) copy-start(bf16[15,48,48]{2,1,0:T(8,128)(2,1)} %param.5) | copy-start | bytes 207364
  15.9 2.1 %copy-start.2 = (bf16[15,3,1,48,8,128]{5,3,0,4,1,2:T(8,128)(2,1)}, bf16[15,3,1,48,8,128]{5,3,0,4,1,2:T(8,128)(2,1)S(1)}, u32[]{:S(2)}) copy-start(bf16[15,3,1,48,8,128]{5,3,0,4,1,2:T(8,128)(2,1)S(1)} %fusion.67) | copy-start | bytes 13271044
  18.0 5.0 %copy-start.5 = (bf16[15,48,48]{2,1,0:T(8,128)(2,1)S(1)}, bf16[15,48,48]{2,1,0:T(8,128)(2,1)}, u32[]{:S(2)}) copy-start(bf16[15,48,48]{2,1,0:T(8,128)(2,1)} %param.6) | copy-start | bytes 207364
  19.8 3.2 %collective-permute-start.2 = (bf16[2,3,1,48,8,7]{3,4,5,2,1,0:T(8,128)(2,1)S(1)}, bf16[2,3,1,48,8,7]{3,4,5,2,1,0:T(8,128)(2,1)S(1)}, u32[]{:S(2)}, u32[]{:S(2)}) collective-permute-start(bf16[2,3,1,48,8,7]{3,4,5,2,1,0:T(8,128)(2,1)S(1)} %copy.85), channel_id=1, source_target_pairs={{0,1},{1,2},{2,3},{3,4},{4,5},{5,6},{6,7},{8,9},{9,10},{10,11},{11... | collective-permute-start | bytes 96776 | tf_op jit(solution)/shard_map/ppermute | solution.py:15
  21.5 5.0 %collective-permute-start.3 = (bf16[2,3,1,48,8,7]{3,4,5,2,1,0:T(8,128)(2,1)S(1)}, bf16[2,3,1,48,8,7]{3,4,5,2,1,0:T(8,128)(2,1)S(1)}, u32[]{:S(2)}, u32[]{:S(2)}) collective-permute-start(bf16[2,3,1,48,8,7]{3,4,5,2,1,0:T(8,128)(2,1)S(1)} %copy.86), channel_id=1, source_target_pairs={{1,0},{2,1},{3,2},{4,3},{5,4},{6,5},{7,6},{9,8},{10,9},{11,10},{12... | collective-permute-start | bytes 96776 | tf_op jit(solution)/shard_map/ppermute | solution.py:17
  33.0 6.6 %slice-start = ((s8[4423680]{0:T(1024)(128)(4,1)}), s8[4194304]{0:T(1024)(128)(4,1)S(1)}, s32[]{:S(2)}) async-start(s8[4423680]{0:T(1024)(128)(4,1)} %bitcast.330), calls=%async_computation.2 | async-start | bytes 8388608
  33.3 2.3 %copy-start = (bf16[15,3,1,48,8,128]{5,3,4,1,2,0:T(8,128)(2,1)}, bf16[15,3,1,48,8,128]{5,3,4,1,2,0:T(8,128)(2,1)S(1)}, u32[]{:S(2)}) copy-start(bf16[15,3,1,48,8,128]{5,3,4,1,2,0:T(8,128)(2,1)S(1)} %get-tuple-element.29) | copy-start | bytes 13271044
  35.6 4.0 %slice-start.1 = ((s8[4423680]{0:T(1024)(128)(4,1)}), s8[229376]{0:T(1024)(128)(4,1)S(1)}, s32[]{:S(2)}) async-start(s8[4423680]{0:T(1024)(128)(4,1)} %bitcast.330), calls=%async_computation.3 | async-start | bytes 458752
  39.6 13.5 %copy-start.3 = (bf16[3,1,48,8,128]{4,3,2,1,0:T(8,128)(2,1)S(1)}, bf16[3,1,48,8,128]{4,3,2,1,0:T(8,128)(2,1)}, u32[]{:S(2)}) copy-start(bf16[3,1,48,8,128]{4,3,2,1,0:T(8,128)(2,1)} %param.7) | copy-start | bytes 884740
  42.2 25.1 %all-to-all-start = ((f32[32,17,128]{2,1,0:T(8,128)}), f32[32,17,128]{2,1,0:T(8,128)S(1)}, u32[]{:S(2)}, u32[]{:S(2)}) async-start(f32[32,17,128]{2,1,0:T(8,128)} %reshape.67), calls=%async_computation | async-start | bytes 786432 | tf_op jit(solution)/shard_map/all_to_all | solution.py:87
  53.6 27.4 %collective-permute-start.4 = (bf16[3,1,48,7,128]{4,2,3,0,1:T(8,128)(2,1)S(1)}, bf16[3,1,48,7,128]{4,2,3,0,1:T(8,128)(2,1)S(1)}, u32[]{:S(2)}, u32[]{:S(2)}) collective-permute-start(bf16[3,1,48,7,128]{4,2,3,0,1:T(8,128)(2,1)S(1)} %get-tuple-element.20), channel_id=1, source_target_pairs={{0,8},{8,16},{16,24},{24,32},{32,40},{40,48},{48,56},{56,64},{64,7... | collective-permute-start | bytes 774152 | tf_op jit(solution)/shard_map/ppermute | solution.py:15
  57.0 24.0 %collective-permute-start.5 = (bf16[3,1,48,7,128]{4,2,3,0,1:T(8,128)(2,1)S(1)}, bf16[3,1,48,7,128]{4,2,3,0,1:T(8,128)(2,1)S(1)}, u32[]{:S(2)}, u32[]{:S(2)}) collective-permute-start(bf16[3,1,48,7,128]{4,2,3,0,1:T(8,128)(2,1)S(1)} %get-tuple-element.21), channel_id=1, source_target_pairs={{8,0},{16,8},{24,16},{32,24},{40,32},{48,40},{56,48},{64,56},{72,6... | collective-permute-start | bytes 774152 | tf_op jit(solution)/shard_map/ppermute | solution.py:17
  67.4 5.8 %collective-permute-start.6 = (f32[17,128]{1,0:T(8,128)S(1)}, f32[17,128]{1,0:T(8,128)S(1)}, u32[]{:S(2)}, u32[]{:S(2)}) collective-permute-start(f32[17,128]{1,0:T(8,128)S(1)} %reduce_sum.9), channel_id=1, source_target_pairs={{0,1},{1,0},{2,3},{3,2},{4,5},{5,4},{6,7},{7,6},{8,9},{9,8},{10,11... | collective-permute-start | bytes 26120 | tf_op jit(solution)/shard_map/ppermute | solution.py:75
  73.2 4.2 %collective-permute-start.7 = (f32[17,128]{1,0:T(8,128)S(1)}, f32[17,128]{1,0:T(8,128)S(1)}, u32[]{:S(2)}, u32[]{:S(2)}) collective-permute-start(f32[17,128]{1,0:T(8,128)S(1)} %add.30), channel_id=1, source_target_pairs={{0,2},{1,3},{2,0},{3,1},{4,6},{5,7},{6,4},{7,5},{8,10},{9,11},{10,... | collective-permute-start | bytes 26120 | tf_op jit(solution)/shard_map/ppermute | solution.py:75
  77.4 5.5 %collective-permute-start.8 = (f32[17,128]{1,0:T(8,128)S(1)}, f32[17,128]{1,0:T(8,128)S(1)}, u32[]{:S(2)}, u32[]{:S(2)}) collective-permute-start(f32[17,128]{1,0:T(8,128)S(1)} %add.31), channel_id=1, source_target_pairs={{0,4},{1,5},{2,6},{3,7},{4,0},{5,1},{6,2},{7,3},{8,12},{9,13},{10,... | collective-permute-start | bytes 26120 | tf_op jit(solution)/shard_map/ppermute | solution.py:75
  83.7 19.2 %all-to-all-start.1 = ((f32[32,17,128]{2,1,0:T(8,128)}), f32[32,17,128]{2,1,0:T(8,128)S(1)}, u32[]{:S(2)}, u32[]{:S(2)}) async-start(f32[32,17,128]{2,1,0:T(8,128)} %broadcast_in_dim.2), calls=%async_computation.1 | async-start | bytes 786432 | tf_op jit(solution)/shard_map/all_to_all | solution.py:89
